TPU v7x, 256 devices: a whole 4x4x8 slice. The times are simulated.
256 devices in a mesh: blk: 64 (over z_hi, x, y, core), path: 4 (over z_lo).
Axes of the slice: x: 4, y: 4, z: 8 (z_hi: 2, z_lo: 4; z = z_hi * 4 + z_lo), core: 2. Of those that a mesh axis runs over, the one named last changes fastest.
Arguments:
- records: bfloat16 [65536, 512], P('blk'), may hold values from -87.98545 to 87.98545
- coefficients: float32 [65536, 64], P('blk', 'path'), may hold values from -6 to 6
- velocity: float32 [65536, 64], P('blk', 'path'), may hold values from -3 to 3
- targets: float32 [65536, 64], P('blk', 'path'), may hold values from -6 to 6
- block_local: int32 [3, 1536], P(None, 'blk'), may hold values from 0 to 1023
- block_count: int32 [3, 64], replicated, may hold values from 1 to 24, 1024 in all within a row
- candidates: bfloat16 [32768, 512], P('blk'), may hold values from -87.98545 to 87.98545
- frequencies: bfloat16 [512, 1024], replicated, may hold values from -0.25 to 0.25
- phases: float32 [1024], replicated, may hold values from -3.140625 to 3.140625
- prior_weight: float32 [1024, 64], P(None, 'path'), may hold values from -6 to 6
Outputs:
- coefficients_out: float32 [65536, 64], P('blk', 'path')
- velocity_out: float32 [65536, 64], P('blk', 'path')
- scores: float32 [32768, 64], P('blk', 'path')
- path_rms: float32 [32768], P('blk')
Inputs may be any that keep to these rules, and one draw needn't show every extreme that they name: `block_count`: each row sums to 1024, and its largest entry is exactly 24. `block_local`: index within the owner's records; a slot at or beyond the owner's count in that step is not used. Used entries of one owner may repeat.
All inputs are finite; a program needn't handle non-finite values.
Results may differ from a plain program's by a relative error of at most 0.0014.
Values may be sent and summed in bfloat16 or wider, within the bound.
No kernel may reach another device: no remote copies, remote signals or barrier semaphores. Data moves between devices by JAX's collectives and lax.ppermute only.
A program may use at most 128 MiB of HBM per device.

v0:
```python
import math

import jax
import jax.numpy as jnp
from jax import lax
from jax.sharding import PartitionSpec as P

NOISE = 0.5
MOMENTUM = 0.9
RATE = 0.3
EPSILON = 1e-06
SIGNAL = 9.0


def passed_along(shard, axis, by):
    length = lax.axis_size(axis)
    return lax.ppermute(shard, axis, [(i, (i + by) % length) for i in range(length)])


def square_norms(row_block):
    widened = row_block.astype(jnp.float32)
    return jnp.sum(widened * widened, axis=1)


def kernel_tile_of(left_rows, left_norms, right_rows, right_norms):
    dot_values = lax.dot_general(
        left_rows, right_rows, (((1,), (1,)), ((), ())), preferred_element_type=jnp.float32
    )
    distance = left_norms[:, None] + right_norms[None, :] - 2.0 * dot_values
    return SIGNAL * jnp.exp(-distance / left_rows.shape[1])


def kernel_apply(left_rows, left_norms, right_rows, right_norms, weights):
    kernel_tile = kernel_tile_of(left_rows, left_norms, right_rows, right_norms)
    return jnp.dot(kernel_tile, weights, precision=lax.Precision.HIGH)


def prior_values(cand_rows, frequencies, phases, prior_weight):
    angles = (
        jnp.dot(cand_rows, frequencies, preferred_element_type=jnp.float32) * math.sqrt(2.0)
        + phases[None, :]
    )
    features = math.sqrt(2.0 * SIGNAL / frequencies.shape[1]) * jnp.cos(angles)
    return jnp.dot(features, prior_weight, precision=lax.Precision.HIGHEST)


def gather_blocks(block, axis):
    length = lax.axis_size(axis)
    flat = block.reshape(1, -1)
    spread = jnp.broadcast_to(flat, (length, flat.shape[1]))
    got = lax.all_to_all(spread, axis, 0, 0, tiled=True)
    return got.reshape((length,) + block.shape)


def gather_stack(block, axis):
    length = lax.axis_size(axis)
    spread = jnp.broadcast_to(block[None], (length,) + block.shape)
    return lax.all_to_all(spread, axis, 0, 0, tiled=True)


def gather_by_permutes(block, axis):
    length = lax.axis_size(axis)
    here = lax.axis_index(axis)
    moved = [block] + [passed_along(block, axis, by) for by in range(1, length)]
    order = (here - jnp.arange(length, dtype=jnp.int32)) % length
    return jnp.take(jnp.stack(moved), order, axis=0)


def sum_to_owners(partial, axis):
    length = lax.axis_size(axis)
    flat = partial.reshape(length, -1)
    got = lax.all_to_all(flat, axis, 0, 0, tiled=True)
    return jnp.sum(got, axis=0).reshape(partial.shape[1:])


def velocity_weights(steps):
    a, b = [], []
    for t in range(steps):
        a.append(sum(MOMENTUM ** u for u in range(1, t + 1)))
        b.append([sum(MOMENTUM ** (u - 1 - s) for u in range(s + 1, t + 1)) for s in range(t)])
    return a, b


def shards(
    records,
    coefficients,
    velocity,
    targets,
    block_local,
    block_count,
    candidates,
    frequencies,
    phases,
    prior_weight,
):
    n_blk = lax.axis_size("blk")
    record_total = records.shape[0] * n_blk
    root_count = jnp.sqrt(jnp.float32(record_total))
    steps, slot_count = block_local.shape
    own_index = lax.axis_index("blk")
    neighbour = passed_along(candidates, "blk", 1)
    work_norms = square_norms(records)
    slot_ids = jnp.arange(slot_count, dtype=jnp.int32)
    paths = coefficients.shape[1]

    n_path = lax.axis_size("path")
    path_index = lax.axis_index("path")
    share = slot_count // n_path
    own_rows = records[block_local.reshape(-1)]
    prior = prior_values(candidates, frequencies, phases, prior_weight)

    share_local = lax.dynamic_slice_in_dim(block_local, path_index * share, share, axis=1)
    share_rows = records[share_local.reshape(-1)]
    gathered = gather_stack(share_rows, "blk")
    gathered, prior = lax.optimization_barrier((gathered, prior))
    all_rows = gathered.reshape(n_blk * steps * share, -1)
    start_weights = jnp.concatenate([coefficients, velocity], axis=1)
    every_weights = gather_by_permutes(start_weights, "path").transpose(1, 0, 2)
    every_weights = every_weights.reshape(start_weights.shape[0], n_path * 2 * paths)
    partial = kernel_apply(all_rows, square_norms(all_rows), records, work_norms, every_weights)
    share_sums = sum_to_owners(partial.reshape(n_blk, steps * share, n_path * 2 * paths), "blk")
    share_sums = share_sums.reshape(steps * share, n_path, 2 * paths).transpose(1, 0, 2)
    got = lax.all_to_all(share_sums, "path", 0, 0, tiled=True)
    start_sums = got.reshape(n_path, steps, share, 2 * paths).transpose(1, 0, 2, 3)
    start_sums = start_sums.reshape(steps, slot_count, 2 * paths)

    pairs = [(t, s) for t in range(steps) for s in range(t)]
    tiles = []
    for t, s in pairs:
        mine = own_rows[t * slot_count:(t + 1) * slot_count]
        theirs = gathered[:, s * share:(s + 1) * share].reshape(n_blk * share, -1)
        tiles.append(kernel_tile_of(mine, square_norms(mine), theirs, square_norms(theirs)))
    tiles = gather_by_permutes(jnp.stack(tiles), "path")
    tiles = tiles.reshape(n_path, len(pairs), slot_count, n_blk, share).transpose(1, 2, 3, 0, 4)
    tiles = tiles.reshape(len(pairs), slot_count, n_blk * slot_count)
    tile_of = {pair: tiles[k] for k, pair in enumerate(pairs)}

    a_weight, b_weight = velocity_weights(steps + 1)
    own_rows_norms = square_norms(own_rows)
    cand_norms = square_norms(candidates)
    neighbour_norms = square_norms(neighbour)
    own_start = kernel_apply(candidates, cand_norms, records, work_norms, start_weights)
    next_start = kernel_apply(neighbour, neighbour_norms, records, work_norms, start_weights)
    own_slots = kernel_tile_of(candidates, cand_norms, own_rows, own_rows_norms)
    next_slots = kernel_tile_of(neighbour, neighbour_norms, own_rows, own_rows_norms)
    weighted_updates = []
    updates = []
    for repeat in range(steps):
        local_rows = block_local[repeat]
        own_count = lax.dynamic_index_in_dim(block_count[repeat], own_index, 0, keepdims=False)
        is_live = slot_ids < own_count
        total = start_sums[repeat, :, :paths]
        if repeat > 0:
            total = total + a_weight[repeat] * start_sums[repeat, :, paths:]
        for earlier in range(repeat):
            cross = jnp.dot(
                tile_of[(repeat, earlier)], updates[earlier], precision=lax.Precision.HIGH
            )
            total = total + b_weight[repeat][earlier] * cross
        product = total / root_count
        gradient = jnp.where(
            is_live[:, None], product + NOISE * coefficients[local_rows] - targets[local_rows], 0.0
        )
        step_update = -RATE * gradient
        velocity = (MOMENTUM * velocity).at[local_rows].add(step_update)
        coefficients = coefficients + velocity
        weighted_updates.append(b_weight[steps][repeat] * step_update)
        if repeat < steps - 1:
            updates.append(gather_blocks(step_update, "blk").reshape(n_blk * slot_count, paths))

    slot_weights = jnp.concatenate(weighted_updates, axis=0)
    own_sum = (
        own_start[:, :paths]
        + a_weight[steps] * own_start[:, paths:]
        + jnp.dot(own_slots, slot_weights, precision=lax.Precision.HIGH)
    )
    next_sum = (
        next_start[:, :paths]
        + a_weight[steps] * next_start[:, paths:]
        + jnp.dot(next_slots, slot_weights, precision=lax.Precision.HIGH)
    )
    first_part = prior + own_sum / root_count
    next_term = next_sum / root_count
    scores = passed_along(first_part, "blk", 2) + passed_along(next_term, "blk", 1)
    squares_local = jnp.sum(scores * scores, axis=1)
    summed = lax.psum(squares_local, "path")
    path_rms = jnp.sqrt(summed / (scores.shape[1] * lax.axis_size("path")) + EPSILON)
    return (coefficients, velocity, scores, path_rms)


def solution(mesh):
    return jax.shard_map(
        shards,
        mesh=mesh,
        in_specs=(
            P("blk", None),
            P("blk", "path"),
            P("blk", "path"),
            P("blk", "path"),
            P(None, "blk"),
            P(),
            P("blk", None),
            P(),
            P(),
            P(None, "path"),
        ),
        out_specs=(P("blk", "path"), P("blk", "path"), P("blk", "path"), P("blk")),
        check_vma=False,
    )
```

profile of v0, /device:TPU:1, one launch (start us, length us, event | category | flops | bytes accessed | tf_op | source)
XLA Modules:
  0.0 233.5 jit_solution(5808928174696182131)
XLA Ops:
  3.1 2.5 %collective-permute-start = (f32[1024,32]{0,1:T(8,128)S(1)}, f32[1024,32]{0,1:T(8,128)}, u32[]{:S(2)}, u32[]{:S(2)}) collective-permute-start(f32[1024,32]{0,1:T(8,128)S(1)} %get-tuple-element.43), channel_id=1, source_target_pairs={{0,1},{1,2},{2,3},{3,0},{4,5},{5,6},{6,7},{7,4},{8,9},{9,10},{10,1... | collective-permute-start | bytes 393224 | tf_op jit(solution)/shard_map/ppermute | solution.py:17
  5.5 3.0 %collective-permute-start.1 = (f32[1024,32]{0,1:T(8,128)S(1)}, f32[1024,32]{0,1:T(8,128)}, u32[]{:S(2)}, u32[]{:S(2)}) collective-permute-start(f32[1024,32]{0,1:T(8,128)S(1)} %get-tuple-element.43), channel_id=1, source_target_pairs={{0,2},{1,3},{2,0},{3,1},{4,6},{5,7},{6,4},{7,5},{8,10},{9,11},{10,... | collective-permute-start | bytes 393224 | tf_op jit(solution)/shard_map/ppermute | solution.py:17
  14.1 14.0 %all-to-all-start = ((bf16[64,18,512]{2,1,0:T(8,128)(2,1)}), bf16[64,18,512]{2,1,0:T(8,128)(2,1)S(1)}, u32[]{:S(2)}, u32[]{:S(2)}) async-start(bf16[64,18,512]{2,1,0:T(8,128)(2,1)} %broadcast_in_dim.57), calls=%async_computation | async-start | bytes 3145728 | tf_op jit(solution)/shard_map/all_to_all | solution.py:58
  32.7 3.1 %fusion.123 = f32[512,1024]{1,0:T(8,128)} fusion(bf16[512,512]{1,0:T(8,128)(2,1)} %param.16, bf16[512,1024]{1,0:T(8,128)(2,1)S(1)} %copy-done), kind=kOutput, calls=%fused_computation.205 | convolution fusion | flops 536870912 | bytes 3670016 | tf_op jit(solution)/shard_map/dot_general | solution.py:40
  37.1 2.1 gather_fusion.4
  42.5 10.8 %fusion.24 = f32[512,16]{0,1:T(8,128)} fusion(f32[1024,16]{0,1:T(8,128)S(1)} %copy-done.9, f32[512,1024]{1,0:T(8,128)} %fusion.123, f32[1024]{0:T(1024)S(1)} %copy-done.26), kind=kOutput, calls=%fused_computation.41 | convolution fusion | flops 102236160 | bytes 2199552 | tf_op jit(solution)/shard_map/dot_general | solution.py:44
  85.5 3.0 %fusion = f32[1152,1024]{1,0:T(8,128)S(1)} fusion(bf16[1152,512]{1,0:T(8,128)(2,1)} %reshape.329, bf16[1024,512]{1,0:T(8,128)(2,1)} %param.10, f32[1024]{0:T(1024)S(1)} %multiply_reduce_fusion.1, f32[1152]{0:T(1024)S(1)} %add.297), kind=kOutput, calls=%fused_computation.14 | convolution fusion | flops 1211498496 | bytes 6955520 | tf_op jit(solution)/shard_map/dot_general | solution.py:26
  88.5 3.1 %fusion.1 = f32[1152,128]{1,0:T(8,128)} fusion(f32[1024,128]{0,1:T(8,128)S(1)} %bitcast.105, f32[1152,1024]{1,0:T(8,128)S(1)} %fusion), kind=kOutput, calls=%fused_computation.15 | convolution fusion | flops 909508608 | bytes 5832704 | tf_op jit(solution)/shard_map/dot_general | solution.py:35
  91.6 12.4 %all-to-all-start.1 = ((f32[64,1,2304]{2,1,0:T(1,128)}), f32[64,1,2304]{2,1,0:T(1,128)}, u32[]{:S(2)}, u32[]{:S(2)}) async-start(f32[64,1,2304]{2,1,0:T(1,128)} %bitcast.11), calls=%async_computation.1 | async-start | bytes 1179648 | tf_op jit(solution)/shard_map/all_to_all | solution.py:72
  107.4 2.3 collective-permute-start.5
  111.7 3.1 %collective-permute-done.3 = f32[3,24,384]{2,1,0:T(8,128)S(1)} collective-permute-done((f32[3,24,384]{2,1,0:T(8,128)S(1)}, f32[3,24,384]{2,1,0:T(8,128)S(1)}, u32[]{:S(2)}, u32[]{:S(2)}) %collective-permute-start.3) | collective-permute-done | bytes 110624 | tf_op jit(solution)/shard_map/ppermute | solution.py:17
  114.8 10.4 %collective-permute-done.4 = f32[3,24,384]{2,1,0:T(8,128)S(1)} collective-permute-done((f32[3,24,384]{2,1,0:T(8,128)S(1)}, f32[3,24,384]{2,1,0:T(8,128)S(1)}, u32[]{:S(2)}, u32[]{:S(2)}) %collective-permute-start.4) | collective-permute-done | bytes 110624 | tf_op jit(solution)/shard_map/ppermute | solution.py:17
  126.0 2.4 %copy.110 = f32[4,3,24,384]{2,0,3,1:T(4,128)} copy(f32[4,3,24,384]{3,2,1,0:T(8,128)S(1)} %gather_fusion.5) | data formatting | bytes 884736 | tf_op jit(solution)/shard_map/jit(_take)/gather | solution.py:66
  128.4 2.3 select_bitcast_fusion
  136.9 6.3 %all-to-all-start.2 = ((f32[4,1,576]{2,1,0:T(1,128)}), f32[4,1,576]{2,1,0:T(1,128)}, u32[]{:S(2)}, u32[]{:S(2)}) async-start(f32[4,1,576]{2,1,0:T(1,128)} %reshape.442), calls=%async_computation.2 | async-start | bytes 20480 | tf_op jit(solution)/shard_map/all_to_all | solution.py:123
  152.5 12.5 %all-to-all-start.3 = ((f32[64,1,384]{2,1,0:T(1,128)}), f32[64,1,384]{2,1,0:T(1,128)S(1)}, u32[]{:S(2)}, u32[]{:S(2)}) async-start(f32[64,1,384]{2,1,0:T(1,128)} %broadcast_in_dim.107), calls=%async_computation.3 | async-start | bytes 196608 | tf_op jit(solution)/shard_map/all_to_all | solution.py:51
  165.8 2.5 %scatter_fusion = f32[1024,16]{1,0:T(8,128)} fusion(f32[1024,16]{1,0:T(8,128)} %copy.105, s32[24]{0:T(128)S(1)} %copy-done.24, f32[24,16]{1,0:T(8,128)S(1)} %copy.106), kind=kCustom, calls=%fused_computation.10 | custom fusion | flops 384 | bytes 4704 | tf_op jit(solution)/shard_map/scatter-add | solution.py:165
  168.3 2.1 broadcast_multiply_fusion
  171.3 6.8 %all-to-all-done.3 = f32[64,1,384]{2,1,0:T(1,128)S(1)} async-done(((f32[64,1,384]{2,1,0:T(1,128)}), f32[64,1,384]{2,1,0:T(1,128)S(1)}, u32[]{:S(2)}, u32[]{:S(2)}) %all-to-all-start.3) | async-done | bytes 98336 | tf_op jit(solution)/shard_map/all_to_all | solution.py:51
  180.7 2.5 %scatter_fusion.1 = f32[1024,16]{1,0:T(8,128)} fusion(f32[1024,16]{1,0:T(8,128)} %get-tuple-element.39, s32[24]{0:T(128)S(1)} %copy-done.22, f32[24,16]{1,0:T(8,128)S(1)} %copy.118), kind=kCustom, calls=%fused_computation.11 | custom fusion | flops 384 | bytes 4704 | tf_op jit(solution)/shard_map/scatter-add | solution.py:165
  188.4 6.0 %all-to-all-start.4 = ((f32[64,1,384]{2,1,0:T(1,128)}), f32[64,1,384]{2,1,0:T(1,128)S(1)}, u32[]{:S(2)}, u32[]{:S(2)}) async-start(f32[64,1,384]{2,1,0:T(1,128)} %broadcast_in_dim.110), calls=%async_computation.4 | async-start | bytes 196608 | tf_op jit(solution)/shard_map/all_to_all | solution.py:51
  196.3 11.2 %all-to-all-done.4 = f32[64,1,384]{2,1,0:T(1,128)S(1)} async-done(((f32[64,1,384]{2,1,0:T(1,128)}), f32[64,1,384]{2,1,0:T(1,128)S(1)}, u32[]{:S(2)}, u32[]{:S(2)}) %all-to-all-start.4) | async-done | bytes 98336 | tf_op jit(solution)/shard_map/all_to_all | solution.py:51
  216.7 8.0 %collective-permute-done.6 = f32[512,16]{0,1:T(8,128)S(1)} collective-permute-done((f32[512,16]{0,1:T(8,128)S(1)}, f32[512,16]{0,1:T(8,128)S(1)}, u32[]{:S(2)}, u32[]{:S(2)}) %collective-permute-start.6) | collective-permute-done | bytes 32800 | tf_op jit(solution)/shard_map/ppermute | solution.py:17
  225.3 7.6 %psum.7 = f32[512]{0:T(512)S(1)} all-reduce(f32[512]{0:T(512)S(1)} %get-tuple-element.28), channel_id=1, replica_groups=mesh['blk'=64,'path'=4] {'path'}, use_global_device_ids=true, to_apply=%region_14.15 | all-reduce | flops 512 | bytes 4096 | tf_op jit(solution)/shard_map/psum | solution.py:186
  (209 shorter events, 92.3 us)
Async XLA Ops:
  0.6 32.0 %copy-start = (bf16[512,1024]{1,0:T(8,128)(2,1)S(1)}, bf16[512,1024]{1,0:T(8,128)(2,1)}, u32[]{:S(2)}) copy-start(bf16[512,1024]{1,0:T(8,128)(2,1)} %param.17) | copy-start | bytes 3145732
  3.1 70.2 %collective-permute-start = (f32[1024,32]{0,1:T(8,128)S(1)}, f32[1024,32]{0,1:T(8,128)}, u32[]{:S(2)}, u32[]{:S(2)}) collective-permute-start(f32[1024,32]{0,1:T(8,128)S(1)} %get-tuple-element.43), channel_id=1, source_target_pairs={{0,1},{1,2},{2,3},{3,0},{4,5},{5,6},{6,7},{7,4},{8,9},{9,10},{10,1... | collective-permute-start | bytes 393224 | tf_op jit(solution)/shard_map/ppermute | solution.py:17
  5.5 67.7 %collective-permute-start.1 = (f32[1024,32]{0,1:T(8,128)S(1)}, f32[1024,32]{0,1:T(8,128)}, u32[]{:S(2)}, u32[]{:S(2)}) collective-permute-start(f32[1024,32]{0,1:T(8,128)S(1)} %get-tuple-element.43), channel_id=1, source_target_pairs={{0,2},{1,3},{2,0},{3,1},{4,6},{5,7},{6,4},{7,5},{8,10},{9,11},{10,... | collective-permute-start | bytes 393224 | tf_op jit(solution)/shard_map/ppermute | solution.py:17
  8.5 64.8 %collective-permute-start.2 = (f32[1024,32]{0,1:T(8,128)S(1)}, f32[1024,32]{0,1:T(8,128)}, u32[]{:S(2)}, u32[]{:S(2)}) collective-permute-start(f32[1024,32]{0,1:T(8,128)S(1)} %get-tuple-element.43), channel_id=1, source_target_pairs={{0,3},{1,0},{2,1},{3,2},{4,7},{5,4},{6,5},{7,6},{8,11},{9,8},{10,9... | collective-permute-start | bytes 393224 | tf_op jit(solution)/shard_map/ppermute | solution.py:17
  10.0 29.4 %copy-start.20 = (s32[24]{0:T(128)}, s32[24]{0:T(128)S(1)}, u32[]{:S(2)}) copy-start(s32[24]{0:T(128)S(1)} %get-tuple-element.56) | copy-start | bytes 292
  10.0 29.4 %copy-start.21 = (s32[24]{0:T(128)}, s32[24]{0:T(128)S(1)}, u32[]{:S(2)}) copy-start(s32[24]{0:T(128)S(1)} %get-tuple-element.57) | copy-start | bytes 292
  14.1 68.0 %all-to-all-start = ((bf16[64,18,512]{2,1,0:T(8,128)(2,1)}), bf16[64,18,512]{2,1,0:T(8,128)(2,1)S(1)}, u32[]{:S(2)}, u32[]{:S(2)}) async-start(bf16[64,18,512]{2,1,0:T(8,128)(2,1)} %broadcast_in_dim.57), calls=%async_computation | async-start | bytes 3145728 | tf_op jit(solution)/shard_map/all_to_all | solution.py:58
  28.1 48.9 %collective-permute-start.7 = (bf16[512,512]{1,0:T(8,128)(2,1)}, bf16[512,512]{1,0:T(8,128)(2,1)}, u32[]{:S(2)}, u32[]{:S(2)}) collective-permute-start(bf16[512,512]{1,0:T(8,128)(2,1)} %param.16), channel_id=1, source_target_pairs={{0,4},{4,8},{8,12},{12,16},{16,20},{20,24},{24,28},{28,32},{32,36}... | collective-permute-start | bytes 1572872 | tf_op jit(solution)/shard_map/ppermute | solution.py:17
  31.3 44.4 %copy-start.29 = (pred[4]{0:T(512)(128)(4,1)}, pred[4]{0:T(512)(128)(4,1)S(1)}, u32[]{:S(2)}) copy-start(pred[4]{0:T(512)(128)(4,1)S(1)} %compare_and_fusion) | copy-start | bytes 16
  35.8 38.5 %copy-start.19 = (s32[1024]{0:T(1024)}, s32[1024]{0:T(1024)S(1)}, u32[]{:S(2)}) copy-start(s32[1024]{0:T(1024)S(1)} %pad_clamp_fusion.4) | copy-start | bytes 12292
  37.1 28.3 %copy-start.30 = (pred[24]{0:T(512)(128)(4,1)}, pred[24]{0:T(512)(128)(4,1)S(1)}, u32[]{:S(2)}) copy-start(pred[24]{0:T(512)(128)(4,1)S(1)} %iota_compare_fusion.2) | copy-start | bytes 76
  39.4 28.6 %copy-start.18 = (s32[1024]{0:T(1024)}, s32[1024]{0:T(1024)S(1)}, u32[]{:S(2)}) copy-start(s32[1024]{0:T(1024)S(1)} %get-tuple-element.60) | copy-start | bytes 12292
  39.4 30.9 %copy-start.17 = (s32[1024]{0:T(1024)}, s32[1024]{0:T(1024)S(1)}, u32[]{:S(2)}) copy-start(s32[1024]{0:T(1024)S(1)} %get-tuple-element.59) | copy-start | bytes 12292
  73.2 31.4 %copy-start.25 = (f32[24]{0:T(128)}, f32[24]{0:T(128)S(1)}, u32[]{:S(2)}) copy-start(f32[24]{0:T(128)S(1)} %get-tuple-element.27) | copy-start | bytes 292
  91.6 39.0 %all-to-all-start.1 = ((f32[64,1,2304]{2,1,0:T(1,128)}), f32[64,1,2304]{2,1,0:T(1,128)}, u32[]{:S(2)}, u32[]{:S(2)}) async-start(f32[64,1,2304]{2,1,0:T(1,128)} %bitcast.11), calls=%async_computation.1 | async-start | bytes 1179648 | tf_op jit(solution)/shard_map/all_to_all | solution.py:72
  106.1 8.7 %collective-permute-start.3 = (f32[3,24,384]{2,1,0:T(8,128)S(1)}, f32[3,24,384]{2,1,0:T(8,128)S(1)}, u32[]{:S(2)}, u32[]{:S(2)}) collective-permute-start(f32[3,24,384]{2,1,0:T(8,128)S(1)} %get-tuple-element.42), channel_id=1, source_target_pairs={{0,1},{1,2},{2,3},{3,0},{4,5},{5,6},{6,7},{7,4},{8,9},{9,10},{10,1... | collective-permute-start | bytes 331784 | tf_op jit(solution)/shard_map/ppermute | solution.py:17
  106.2 19.1 %collective-permute-start.4 = (f32[3,24,384]{2,1,0:T(8,128)S(1)}, f32[3,24,384]{2,1,0:T(8,128)S(1)}, u32[]{:S(2)}, u32[]{:S(2)}) collective-permute-start(f32[3,24,384]{2,1,0:T(8,128)S(1)} %get-tuple-element.42), channel_id=1, source_target_pairs={{0,2},{1,3},{2,0},{3,1},{4,6},{5,7},{6,4},{7,5},{8,10},{9,11},{10,... | collective-permute-start | bytes 331784 | tf_op jit(solution)/shard_map/ppermute | solution.py:17
  107.4 17.8 %collective-permute-start.5 = (f32[3,24,384]{2,1,0:T(8,128)S(1)}, f32[3,24,384]{2,1,0:T(8,128)S(1)}, u32[]{:S(2)}, u32[]{:S(2)}) collective-permute-start(f32[3,24,384]{2,1,0:T(8,128)S(1)} %get-tuple-element.42), channel_id=1, source_target_pairs={{0,3},{1,0},{2,1},{3,2},{4,7},{5,4},{6,5},{7,6},{8,11},{9,8},{10,9... | collective-permute-start | bytes 331784 | tf_op jit(solution)/shard_map/ppermute | solution.py:17
  136.9 11.7 %all-to-all-start.2 = ((f32[4,1,576]{2,1,0:T(1,128)}), f32[4,1,576]{2,1,0:T(1,128)}, u32[]{:S(2)}, u32[]{:S(2)}) async-start(f32[4,1,576]{2,1,0:T(1,128)} %reshape.442), calls=%async_computation.2 | async-start | bytes 20480 | tf_op jit(solution)/shard_map/all_to_all | solution.py:123
  150.7 28.0 %copy-start.11 = (f32[24,16]{0,1:T(8,128)S(1)}, f32[24,16]{0,1:T(8,128)}, u32[]{:S(2)}) copy-start(f32[24,16]{0,1:T(8,128)} %copy.117) | copy-start | bytes 4612
  152.5 25.6 %all-to-all-start.3 = ((f32[64,1,384]{2,1,0:T(1,128)}), f32[64,1,384]{2,1,0:T(1,128)S(1)}, u32[]{:S(2)}, u32[]{:S(2)}) async-start(f32[64,1,384]{2,1,0:T(1,128)} %broadcast_in_dim.107), calls=%async_computation.3 | async-start | bytes 196608 | tf_op jit(solution)/shard_map/all_to_all | solution.py:51
  188.4 19.1 %all-to-all-start.4 = ((f32[64,1,384]{2,1,0:T(1,128)}), f32[64,1,384]{2,1,0:T(1,128)S(1)}, u32[]{:S(2)}, u32[]{:S(2)}) async-start(f32[64,1,384]{2,1,0:T(1,128)} %broadcast_in_dim.110), calls=%async_computation.4 | async-start | bytes 196608 | tf_op jit(solution)/shard_map/all_to_all | solution.py:51
  210.8 6.0 %collective-permute-start.8 = (f32[512,16]{0,1:T(8,128)S(1)}, f32[512,16]{0,1:T(8,128)S(1)}, u32[]{:S(2)}, u32[]{:S(2)}) collective-permute-start(f32[512,16]{0,1:T(8,128)S(1)} %fusion.54), channel_id=1, source_target_pairs={{0,4},{4,8},{8,12},{12,16},{16,20},{20,24},{24,28},{28,32},{32,36}... | collective-permute-start | bytes 98312 | tf_op jit(solution)/shard_map/ppermute | solution.py:17
  212.4 12.2 %collective-permute-start.6 = (f32[512,16]{0,1:T(8,128)S(1)}, f32[512,16]{0,1:T(8,128)S(1)}, u32[]{:S(2)}, u32[]{:S(2)}) collective-permute-start(f32[512,16]{0,1:T(8,128)S(1)} %fusion.56), channel_id=1, source_target_pairs={{0,8},{4,12},{8,16},{12,20},{16,24},{20,28},{24,32},{28,36},{32,40... | collective-permute-start | bytes 98312 | tf_op jit(solution)/shard_map/ppermute | solution.py:17
  (26 other events, 276.9 us)
where the time goes:
time: 236 us; the launch traced here: 234 us
  starting transfers between devices  63.7 us (27%)
  local copies, waits for them, and re-layouts  48.7 us (21%)
  matrix products  40 us (17%)
  waiting for transfers between devices  39.6 us (17%)
  other arithmetic  32.5 us (14%)
  blocking collectives  7.61 us (3%)
    ppermute x9, waiting for transfers between devices, passed_along(): lax.ppermute(shard, axis, [(i, (i + by) % length) for i in range(length)])  21.5 us
    all_to_all x2, starting transfers between devices, gather_blocks(): got = lax.all_to_all(spread, axis, 0, 0, tiled=True)  18.5 us
    all_to_all x2, waiting for transfers between devices, gather_blocks(): got = lax.all_to_all(spread, axis, 0, 0, tiled=True)  18 us
    all_to_all x1, starting transfers between devices, gather_stack(): return lax.all_to_all(spread, axis, 0, 0, tiled=True)  14 us
    ppermute x9, starting transfers between devices, passed_along(): lax.ppermute(shard, axis, [(i, (i + by) % length) for i in range(length)])  12.6 us
    all_to_all x1, starting transfers between devices, sum_to_owners(): got = lax.all_to_all(flat, axis, 0, 0, tiled=True)  12.4 us
    dot_general x8, matrix products, kernel_tile_of(): lax.dot_general(left_rows, right_rows, (((1,), (1,)), ((), ())), preferre...  11.3 us
    dot_general x1, matrix products, prior_values(): return jnp.dot(features, prior_weight, precision=lax.Precision.HIGHEST)  10.8 us
  transfers between devices with their start and end apart: 14, of which 5 were waited for; matrix products, arithmetic and copies ran while one was open for 36% of the time, Pallas kernels for 0%

commit v1 on v0

--- a/solution.py
+++ b/solution.py
@@ -107,17 +107,16 @@
     path_index = lax.axis_index("path")
     share = slot_count // n_path
     own_rows = records[block_local.reshape(-1)]
-    prior = prior_values(candidates, frequencies, phases, prior_weight)
 
     share_local = lax.dynamic_slice_in_dim(block_local, path_index * share, share, axis=1)
     share_rows = records[share_local.reshape(-1)]
     gathered = gather_stack(share_rows, "blk")
-    gathered, prior = lax.optimization_barrier((gathered, prior))
     all_rows = gathered.reshape(n_blk * steps * share, -1)
     start_weights = jnp.concatenate([coefficients, velocity], axis=1)
     every_weights = gather_by_permutes(start_weights, "path").transpose(1, 0, 2)
     every_weights = every_weights.reshape(start_weights.shape[0], n_path * 2 * paths)
     partial = kernel_apply(all_rows, square_norms(all_rows), records, work_norms, every_weights)
+    partial, candidates, neighbour = lax.optimization_barrier((partial, candidates, neighbour))
     share_sums = sum_to_owners(partial.reshape(n_blk, steps * share, n_path * 2 * paths), "blk")
     share_sums = share_sums.reshape(steps * share, n_path, 2 * paths).transpose(1, 0, 2)
     got = lax.all_to_all(share_sums, "path", 0, 0, tiled=True)
@@ -136,6 +135,7 @@
     tile_of = {pair: tiles[k] for k, pair in enumerate(pairs)}
 
     a_weight, b_weight = velocity_weights(steps + 1)
+    prior = prior_values(candidates, frequencies, phases, prior_weight)
     own_rows_norms = square_norms(own_rows)
     cand_norms = square_norms(candidates)
     neighbour_norms = square_norms(neighbour)

time: 236 us -> 253 us (1.072)
  starting transfers between devices: 63.7 us -> 73.1 us
  matrix products: 40 us -> 45.3 us
  other arithmetic: 32.5 us -> 37.1 us
    all_to_all x1, starting transfers between devices: 12.4 us -> 23.4 us  [sum_to_owners(): got = lax.all_to_all(flat, axis, 0, 0, tiled=True)]
    dot_general x8, matrix products: 11.3 us -> 16.2 us  [kernel_tile_of(): lax.dot_general(left_rows, right_rows, (((1,), (1,)), ((), ())), preferre...]
    unnamed x84 -> x94, local copies, waits for them, and re-layouts: 8.13 us -> 5.13 us
    all_to_all x2, starting transfers between devices: 18.5 us -> 15.6 us  [gather_blocks(): got = lax.all_to_all(spread, axis, 0, 0, tiled=True)]
    add x3, local copies, waits for them, and re-layouts: 0.4 us -> 3.08 us  [kernel_tile_of(): distance = left_norms[:, None] + right_norms[None, :] - 2.0 * dot_values]
  transfers between devices with their start and end apart: 14 -> 14, of which waited for: 5 -> 4; matrix products, arithmetic and copies ran while one was open for 36% -> 42% of each run, Pallas kernels for 0% -> 0%
where the time goes in v1:
time: 253 us; the launch traced here: 250 us
  starting transfers between devices  73.1 us (29%)
  local copies, waits for them, and re-layouts  46.8 us (18%)
  matrix products  45.3 us (18%)
  waiting for transfers between devices  39.1 us (15%)
  other arithmetic  37.1 us (15%)
  blocking collectives  7.67 us (3%)
    all_to_all x1, starting transfers between devices, sum_to_owners(): got = lax.all_to_all(flat, axis, 0, 0, tiled=True)  23.4 us
    ppermute x9, waiting for transfers between devices, passed_along(): lax.ppermute(shard, axis, [(i, (i + by) % length) for i in range(length)])  20.7 us
    all_to_all x2, waiting for transfers between devices, gather_blocks(): got = lax.all_to_all(spread, axis, 0, 0, tiled=True)  18.4 us
    dot_general x8, matrix products, kernel_tile_of(): lax.dot_general(left_rows, right_rows, (((1,), (1,)), ((), ())), preferre...  16.2 us
    all_to_all x1, starting transfers between devices, gather_stack(): return lax.all_to_all(spread, axis, 0, 0, tiled=True)  15.7 us
    all_to_all x2, starting transfers between devices, gather_blocks(): got = lax.all_to_all(spread, axis, 0, 0, tiled=True)  15.6 us
    ppermute x9, starting transfers between devices, passed_along(): lax.ppermute(shard, axis, [(i, (i + by) % length) for i in range(length)])  12.5 us
    dot_general x1, matrix products, prior_values(): return jnp.dot(features, prior_weight, precision=lax.Precision.HIGHEST)  9.14 us
  transfers between devices with their start and end apart: 14, of which 4 were waited for; matrix products, arithmetic and copies ran while one was open for 42% of the time, Pallas kernels for 0%

profile of v1, /device:TPU:1, one launch (start us, length us, event | category | flops | bytes accessed | tf_op | source)
XLA Modules:
  0.0 250.3 jit_solution(12980364388344656301)
XLA Ops:
  5.6 15.7 %all-to-all-start = ((bf16[64,18,512]{2,1,0:T(8,128)(2,1)}), bf16[64,18,512]{2,1,0:T(8,128)(2,1)S(1)}, u32[]{:S(2)}, u32[]{:S(2)}) async-start(bf16[64,18,512]{2,1,0:T(8,128)(2,1)} %broadcast_in_dim.57), calls=%async_computation | async-start | bytes 3145728 | tf_op jit(solution)/shard_map/all_to_all | solution.py:58
  25.0 2.5 collective-permute-start.3
  51.1 15.4 %collective-permute-done.1 = f32[1024,32]{0,1:T(8,128)} collective-permute-done((f32[1024,32]{0,1:T(8,128)S(1)}, f32[1024,32]{0,1:T(8,128)}, u32[]{:S(2)}, u32[]{:S(2)}) %collective-permute-start.1) | collective-permute-done | bytes 131104 | tf_op jit(solution)/shard_map/ppermute | solution.py:17
  83.5 3.1 %collective-permute-start.4 = (f32[3,24,384]{2,1,0:T(8,128)}, f32[3,24,384]{2,1,0:T(8,128)}, u32[]{:S(2)}, u32[]{:S(2)}) collective-permute-start(f32[3,24,384]{2,1,0:T(8,128)} %get-tuple-element.44), channel_id=1, source_target_pairs={{0,1},{1,2},{2,3},{3,0},{4,5},{5,6},{6,7},{7,4},{8,9},{9,10},{10,1... | collective-permute-start | bytes 331784 | tf_op jit(solution)/shard_map/ppermute | solution.py:17
  90.5 3.0 %fusion = f32[1152,1024]{1,0:T(8,128)S(1)} fusion(bf16[1152,512]{1,0:T(8,128)(2,1)} %reshape.329, bf16[1024,512]{1,0:T(8,128)(2,1)} %param.10, f32[1024]{0:T(1024)S(1)} %copy-done.33, f32[1152]{0:T(1024)S(1)} %add.295), kind=kOutput, calls=%fused_computation.14 | convolution fusion | flops 1211498496 | bytes 6955520 | tf_op jit(solution)/shard_map/dot_general | solution.py:26
  93.5 3.1 %fusion.1 = f32[1152,128]{1,0:T(8,128)} fusion(f32[1024,128]{0,1:T(8,128)S(1)} %bitcast.92, f32[1152,1024]{1,0:T(8,128)S(1)} %fusion), kind=kOutput, calls=%fused_computation.15 | convolution fusion | flops 909508608 | bytes 5832704 | tf_op jit(solution)/shard_map/dot_general | solution.py:35
  97.9 3.1 %fusion.118 = f32[512,1024]{1,0:T(8,128)} fusion(bf16[512,512]{1,0:T(8,128)(2,1)} %collective-permute-done.3, bf16[1024,512]{1,0:T(8,128)(2,1)S(1)} %copy-done.1), kind=kOutput, calls=%fused_computation.198 | convolution fusion | flops 536870912 | bytes 3670016 | tf_op jit(solution)/shard_map/dot_general | solution.py:26
  104.0 23.4 %all-to-all-start.1 = ((f32[64,1,2304]{2,1,0:T(1,128)}), f32[64,1,2304]{2,1,0:T(1,128)}, u32[]{:S(2)}, u32[]{:S(2)}) async-start(f32[64,1,2304]{2,1,0:T(1,128)} %bitcast.11), calls=%async_computation.1 | async-start | bytes 1179648 | tf_op jit(solution)/shard_map/all_to_all | solution.py:72
  127.4 3.7 %fusion.8 = f32[512,32]{0,1:T(8,128)} fusion(f32[1024,32]{0,1:T(8,128)S(1)} %copy-done.15, f32[512,1024]{1,0:T(8,128)} %fusion.118, f32[512]{0:T(512)S(1)} %multiply_reduce_fusion.2, f32[1024]{0:T(1024)S(1)} %copy-done.34), kind=kOutput, calls=%fused_computation.24 | convolution fusion | flops 103809024 | bytes 2299904 | tf_op jit(solution)/shard_map/dot_general | solution.py:35
  135.1 3.1 %fusion.116 = f32[512,1024]{1,0:T(8,128)} fusion(bf16[512,512]{1,0:T(8,128)(2,1)} %param.16, bf16[512,1024]{1,0:T(8,128)(2,1)S(1)} %copy-done), kind=kOutput, calls=%fused_computation.196 | convolution fusion | flops 536870912 | bytes 3670016 | tf_op jit(solution)/shard_map/dot_general | solution.py:40
  142.0 2.4 copy.110
  144.4 2.3 select_bitcast_fusion
  148.9 6.0 %all-to-all-start.2 = ((f32[4,1,576]{2,1,0:T(1,128)}), f32[4,1,576]{2,1,0:T(1,128)S(1)}, u32[]{:S(2)}, u32[]{:S(2)}) async-start(f32[4,1,576]{2,1,0:T(1,128)} %reshape.442), calls=%async_computation.2 | async-start | bytes 20480 | tf_op jit(solution)/shard_map/all_to_all | solution.py:122
  163.7 10.3 %all-to-all-start.3 = ((f32[64,1,384]{2,1,0:T(1,128)}), f32[64,1,384]{2,1,0:T(1,128)S(1)}, u32[]{:S(2)}, u32[]{:S(2)}) async-start(f32[64,1,384]{2,1,0:T(1,128)} %broadcast_in_dim.107), calls=%async_computation.3 | async-start | bytes 196608 | tf_op jit(solution)/shard_map/all_to_all | solution.py:51
  174.2 2.5 %scatter_fusion = f32[1024,16]{1,0:T(8,128)} fusion(f32[1024,16]{1,0:T(8,128)} %copy.105, s32[24]{0:T(128)S(1)} %copy-done.31, f32[24,16]{1,0:T(8,128)S(1)} %copy.106), kind=kCustom, calls=%fused_computation.10 | custom fusion | flops 384 | bytes 4704 | tf_op jit(solution)/shard_map/scatter-add | solution.py:165
  179.6 7.6 %all-to-all-done.3 = f32[64,1,384]{2,1,0:T(1,128)S(1)} async-done(((f32[64,1,384]{2,1,0:T(1,128)}), f32[64,1,384]{2,1,0:T(1,128)S(1)}, u32[]{:S(2)}, u32[]{:S(2)}) %all-to-all-start.3) | async-done | bytes 98336 | tf_op jit(solution)/shard_map/all_to_all | solution.py:51
  189.3 2.5 %scatter_fusion.1 = f32[1024,16]{1,0:T(8,128)} fusion(f32[1024,16]{1,0:T(8,128)} %get-tuple-element.41, s32[24]{0:T(128)S(1)} %copy-done.29, f32[24,16]{1,0:T(8,128)S(1)} %copy.118), kind=kCustom, calls=%fused_computation.11 | custom fusion | flops 384 | bytes 4704 | tf_op jit(solution)/shard_map/scatter-add | solution.py:165
  195.2 5.3 %all-to-all-start.4 = ((f32[64,1,384]{2,1,0:T(1,128)}), f32[64,1,384]{2,1,0:T(1,128)S(1)}, u32[]{:S(2)}, u32[]{:S(2)}) async-start(f32[64,1,384]{2,1,0:T(1,128)} %broadcast_in_dim.110), calls=%async_computation.4 | async-start | bytes 196608 | tf_op jit(solution)/shard_map/all_to_all | solution.py:51
  200.5 2.3 fusion.65
  202.8 10.8 %all-to-all-done.4 = f32[64,1,384]{2,1,0:T(1,128)S(1)} async-done(((f32[64,1,384]{2,1,0:T(1,128)}), f32[64,1,384]{2,1,0:T(1,128)S(1)}, u32[]{:S(2)}, u32[]{:S(2)}) %all-to-all-start.4) | async-done | bytes 98336 | tf_op jit(solution)/shard_map/all_to_all | solution.py:51
  220.1 9.1 %fusion.57 = f32[512,16]{0,1:T(8,128)S(1)} fusion(f32[512,16]{0,1:T(8,128)S(1)} %fusion.61, f32[1024,16]{0,1:T(8,128)S(1)} %copy-done.20, f32[512,1024]{1,0:T(8,128)S(1)} %copy-done.2, f32[1024]{0:T(1024)S(1)} %copy-done.32), kind=kOutput, calls=%fused_computation.79 | convolution fusion | flops 102244352 | bytes 2232320 | tf_op jit(solution)/shard_map/dot_general | solution.py:44
  229.7 2.5 scatter_fusion.2
  236.2 5.3 %collective-permute-done.7 = f32[512,16]{0,1:T(8,128)S(1)} collective-permute-done((f32[512,16]{0,1:T(8,128)S(1)}, f32[512,16]{0,1:T(8,128)S(1)}, u32[]{:S(2)}, u32[]{:S(2)}) %collective-permute-start.7) | collective-permute-done | bytes 32800 | tf_op jit(solution)/shard_map/ppermute | solution.py:17
  242.1 7.7 %psum.7 = f32[512]{0:T(512)S(1)} all-reduce(f32[512]{0:T(512)S(1)} %get-tuple-element.30), channel_id=1, replica_groups=mesh['blk'=64,'path'=4] {'path'}, use_global_device_ids=true, to_apply=%region_14.15 | all-reduce | flops 512 | bytes 4096 | tf_op jit(solution)/shard_map/psum | solution.py:186
  (219 shorter events, 96.5 us)
Async XLA Ops:
  0.6 134.5 %copy-start = (bf16[512,1024]{1,0:T(8,128)(2,1)S(1)}, bf16[512,1024]{1,0:T(8,128)(2,1)}, u32[]{:S(2)}) copy-start(bf16[512,1024]{1,0:T(8,128)(2,1)} %param.17) | copy-start | bytes 3145732
  1.5 33.1 %copy-start.26 = (s32[24]{0:T(128)}, s32[24]{0:T(128)S(1)}, u32[]{:S(2)}) copy-start(s32[24]{0:T(128)S(1)} %get-tuple-element.58) | copy-start | bytes 292
  1.5 33.1 %copy-start.28 = (s32[24]{0:T(128)}, s32[24]{0:T(128)S(1)}, u32[]{:S(2)}) copy-start(s32[24]{0:T(128)S(1)} %get-tuple-element.59) | copy-start | bytes 292
  5.6 24.1 %copy-start.38 = (s32[3,64]{1,0:T(4,128)S(1)}, s32[3,64]{1,0:T(4,128)}, u32[]{:S(2)}) copy-start(s32[3,64]{1,0:T(4,128)} %param.15) | copy-start | bytes 2308
  5.6 64.6 %all-to-all-start = ((bf16[64,18,512]{2,1,0:T(8,128)(2,1)}), bf16[64,18,512]{2,1,0:T(8,128)(2,1)S(1)}, u32[]{:S(2)}, u32[]{:S(2)}) async-start(bf16[64,18,512]{2,1,0:T(8,128)(2,1)} %broadcast_in_dim.57), calls=%async_computation | async-start | bytes 3145728 | tf_op jit(solution)/shard_map/all_to_all | solution.py:58
  21.4 45.0 %copy-start.14 = (f32[1024,32]{0,1:T(8,128)}, f32[1024,32]{0,1:T(8,128)S(1)}, u32[]{:S(2)}) copy-start(f32[1024,32]{0,1:T(8,128)S(1)} %get-tuple-element.45) | copy-start | bytes 393220
  21.4 29.7 %collective-permute-start = (f32[1024,32]{0,1:T(8,128)S(1)}, f32[1024,32]{0,1:T(8,128)}, u32[]{:S(2)}, u32[]{:S(2)}) collective-permute-start(f32[1024,32]{0,1:T(8,128)S(1)} %get-tuple-element.45), channel_id=1, source_target_pairs={{0,1},{1,2},{2,3},{3,0},{4,5},{5,6},{6,7},{7,4},{8,9},{9,10},{10,1... | collective-permute-start | bytes 393224 | tf_op jit(solution)/shard_map/ppermute | solution.py:17
  22.2 44.2 %collective-permute-start.1 = (f32[1024,32]{0,1:T(8,128)S(1)}, f32[1024,32]{0,1:T(8,128)}, u32[]{:S(2)}, u32[]{:S(2)}) collective-permute-start(f32[1024,32]{0,1:T(8,128)S(1)} %get-tuple-element.45), channel_id=1, source_target_pairs={{0,2},{1,3},{2,0},{3,1},{4,6},{5,7},{6,4},{7,5},{8,10},{9,11},{10,... | collective-permute-start | bytes 393224 | tf_op jit(solution)/shard_map/ppermute | solution.py:17
  23.4 43.0 %collective-permute-start.2 = (f32[1024,32]{0,1:T(8,128)S(1)}, f32[1024,32]{0,1:T(8,128)}, u32[]{:S(2)}, u32[]{:S(2)}) collective-permute-start(f32[1024,32]{0,1:T(8,128)S(1)} %get-tuple-element.45), channel_id=1, source_target_pairs={{0,3},{1,0},{2,1},{3,2},{4,7},{5,4},{6,5},{7,6},{8,11},{9,8},{10,9... | collective-permute-start | bytes 393224 | tf_op jit(solution)/shard_map/ppermute | solution.py:17
  25.0 71.6 %collective-permute-start.3 = (bf16[512,512]{1,0:T(8,128)(2,1)}, bf16[512,512]{1,0:T(8,128)(2,1)}, u32[]{:S(2)}, u32[]{:S(2)}) collective-permute-start(bf16[512,512]{1,0:T(8,128)(2,1)} %param.16), channel_id=1, source_target_pairs={{0,4},{4,8},{8,12},{12,16},{16,20},{20,24},{24,28},{28,32},{32,36}... | collective-permute-start | bytes 1572872 | tf_op jit(solution)/shard_map/ppermute | solution.py:17
  29.7 37.8 %copy-start.11 = (bf16[72,512]{1,0:T(8,128)(2,1)}, bf16[72,512]{1,0:T(8,128)(2,1)S(1)}, u32[]{:S(2)}) copy-start(bf16[72,512]{1,0:T(8,128)(2,1)S(1)} %gather_fusion.4) | copy-start | bytes 221188
  39.4 27.0 %copy-start.7 = (f32[1024,16]{1,0:T(8,128)}, f32[1024,16]{1,0:T(8,128)S(1)}, u32[]{:S(2)}) copy-start(f32[1024,16]{1,0:T(8,128)S(1)} %copy.107) | copy-start | bytes 196612
  83.5 56.7 %collective-permute-start.4 = (f32[3,24,384]{2,1,0:T(8,128)}, f32[3,24,384]{2,1,0:T(8,128)}, u32[]{:S(2)}, u32[]{:S(2)}) collective-permute-start(f32[3,24,384]{2,1,0:T(8,128)} %get-tuple-element.44), channel_id=1, source_target_pairs={{0,1},{1,2},{2,3},{3,0},{4,5},{5,6},{6,7},{7,4},{8,9},{9,10},{10,1... | collective-permute-start | bytes 331784 | tf_op jit(solution)/shard_map/ppermute | solution.py:17
  86.6 53.7 %collective-permute-start.5 = (f32[3,24,384]{2,1,0:T(8,128)}, f32[3,24,384]{2,1,0:T(8,128)}, u32[]{:S(2)}, u32[]{:S(2)}) collective-permute-start(f32[3,24,384]{2,1,0:T(8,128)} %get-tuple-element.44), channel_id=1, source_target_pairs={{0,2},{1,3},{2,0},{3,1},{4,6},{5,7},{6,4},{7,5},{8,10},{9,11},{10,... | collective-permute-start | bytes 331784 | tf_op jit(solution)/shard_map/ppermute | solution.py:17
  88.0 52.3 %collective-permute-start.6 = (f32[3,24,384]{2,1,0:T(8,128)}, f32[3,24,384]{2,1,0:T(8,128)}, u32[]{:S(2)}, u32[]{:S(2)}) collective-permute-start(f32[3,24,384]{2,1,0:T(8,128)} %get-tuple-element.44), channel_id=1, source_target_pairs={{0,3},{1,0},{2,1},{3,2},{4,7},{5,4},{6,5},{7,6},{8,11},{9,8},{10,9... | collective-permute-start | bytes 331784 | tf_op jit(solution)/shard_map/ppermute | solution.py:17
  102.2 25.2 %copy-start.15 = (f32[1024,32]{0,1:T(8,128)S(1)}, f32[1024,32]{0,1:T(8,128)}, u32[]{:S(2)}) copy-start(f32[1024,32]{0,1:T(8,128)} %copy-done.14) | copy-start | bytes 393220
  102.2 25.2 %copy-start.34 = (f32[1024]{0:T(1024)S(1)}, f32[1024]{0:T(1024)}, u32[]{:S(2)}) copy-start(f32[1024]{0:T(1024)} %multiply_reduce_fusion.1) | copy-start | bytes 12292
  104.0 42.6 %all-to-all-start.1 = ((f32[64,1,2304]{2,1,0:T(1,128)}), f32[64,1,2304]{2,1,0:T(1,128)}, u32[]{:S(2)}, u32[]{:S(2)}) async-start(f32[64,1,2304]{2,1,0:T(1,128)} %bitcast.11), calls=%async_computation.1 | async-start | bytes 1179648 | tf_op jit(solution)/shard_map/all_to_all | solution.py:72
  148.9 12.2 %all-to-all-start.2 = ((f32[4,1,576]{2,1,0:T(1,128)}), f32[4,1,576]{2,1,0:T(1,128)S(1)}, u32[]{:S(2)}, u32[]{:S(2)}) async-start(f32[4,1,576]{2,1,0:T(1,128)} %reshape.442), calls=%async_computation.2 | async-start | bytes 20480 | tf_op jit(solution)/shard_map/all_to_all | solution.py:122
  162.4 25.2 %copy-start.5 = (f32[24,1536]{0,1:T(8,128)S(1)}, f32[24,1536]{0,1:T(8,128)}, u32[]{:S(2)}) copy-start(f32[24,1536]{0,1:T(8,128)} %squeeze.40) | copy-start | bytes 442372
  163.7 23.4 %all-to-all-start.3 = ((f32[64,1,384]{2,1,0:T(1,128)}), f32[64,1,384]{2,1,0:T(1,128)S(1)}, u32[]{:S(2)}, u32[]{:S(2)}) async-start(f32[64,1,384]{2,1,0:T(1,128)} %broadcast_in_dim.107), calls=%async_computation.3 | async-start | bytes 196608 | tf_op jit(solution)/shard_map/all_to_all | solution.py:51
  195.2 18.4 %all-to-all-start.4 = ((f32[64,1,384]{2,1,0:T(1,128)}), f32[64,1,384]{2,1,0:T(1,128)S(1)}, u32[]{:S(2)}, u32[]{:S(2)}) async-start(f32[64,1,384]{2,1,0:T(1,128)} %broadcast_in_dim.110), calls=%async_computation.4 | async-start | bytes 196608 | tf_op jit(solution)/shard_map/all_to_all | solution.py:51
  218.4 17.8 %collective-permute-start.8 = (f32[512,16]{0,1:T(8,128)S(1)}, f32[512,16]{0,1:T(8,128)S(1)}, u32[]{:S(2)}, u32[]{:S(2)}) collective-permute-start(f32[512,16]{0,1:T(8,128)S(1)} %fusion.60), channel_id=1, source_target_pairs={{0,4},{4,8},{8,12},{12,16},{16,20},{20,24},{24,28},{28,32},{32,36}... | collective-permute-start | bytes 98312 | tf_op jit(solution)/shard_map/ppermute | solution.py:17
  229.2 12.2 %collective-permute-start.7 = (f32[512,16]{0,1:T(8,128)S(1)}, f32[512,16]{0,1:T(8,128)S(1)}, u32[]{:S(2)}, u32[]{:S(2)}) collective-permute-start(f32[512,16]{0,1:T(8,128)S(1)} %fusion.57), channel_id=1, source_target_pairs={{0,8},{4,12},{8,16},{12,20},{16,24},{20,28},{24,32},{28,36},{32,40... | collective-permute-start | bytes 98312 | tf_op jit(solution)/shard_map/ppermute | solution.py:17
  (31 other events, 293.8 us)

commit v2 on v0

--- a/solution.py
+++ b/solution.py
@@ -98,7 +98,6 @@
     root_count = jnp.sqrt(jnp.float32(record_total))
     steps, slot_count = block_local.shape
     own_index = lax.axis_index("blk")
-    neighbour = passed_along(candidates, "blk", 1)
     work_norms = square_norms(records)
     slot_ids = jnp.arange(slot_count, dtype=jnp.int32)
     paths = coefficients.shape[1]
@@ -118,6 +117,8 @@
     every_weights = gather_by_permutes(start_weights, "path").transpose(1, 0, 2)
     every_weights = every_weights.reshape(start_weights.shape[0], n_path * 2 * paths)
     partial = kernel_apply(all_rows, square_norms(all_rows), records, work_norms, every_weights)
+    partial, late_candidates = lax.optimization_barrier((partial, candidates))
+    neighbour = passed_along(late_candidates, "blk", 1)
     share_sums = sum_to_owners(partial.reshape(n_blk, steps * share, n_path * 2 * paths), "blk")
     share_sums = share_sums.reshape(steps * share, n_path, 2 * paths).transpose(1, 0, 2)
     got = lax.all_to_all(share_sums, "path", 0, 0, tiled=True)

time: 236 us -> 226 us (0.958)
  waiting for transfers between devices: 39.6 us -> 25.9 us
  local copies, waits for them, and re-layouts: 48.7 us -> 59.4 us
  matrix products: 40 us -> 31.8 us
    ppermute x9, waiting for transfers between devices: 21.5 us -> 6.73 us  [passed_along(): lax.ppermute(shard, axis, [(i, (i + by) % length) for i in range(length)])]
    squeeze x3, local copies, waits for them, and re-layouts: 2.08 us -> 6.6 us  [shards(): tile_of = {pair: tiles[k] for k, pair in enumerate(pairs)}]
    dot_general x8, matrix products: 11.3 us -> 6.79 us  [kernel_tile_of(): lax.dot_general(left_rows, right_rows, (((1,), (1,)), ((), ())), preferre...]
    slice x4, local copies, waits for them, and re-layouts: 3.24 us -> 7.28 us  [shards(): tile_of = {pair: tiles[k] for k, pair in enumerate(pairs)}]
    all_to_all x1, waiting for transfers between devices: 0.01 us -> 3.46 us  [shards(): got = lax.all_to_all(share_sums, 'path', 0, 0, tiled=True)]
    all_to_all x1, starting transfers between devices: 6.31 us -> 3.25 us  [shards(): got = lax.all_to_all(share_sums, 'path', 0, 0, tiled=True)]
    all_to_all x2, starting transfers between devices: 18.5 us -> 21.4 us  [gather_blocks(): got = lax.all_to_all(spread, axis, 0, 0, tiled=True)]
    gather x3, local copies, waits for them, and re-layouts: 4.46 us -> 7.27 us  [gather_by_permutes(): return jnp.take(jnp.stack(moved), order, axis=0)]
  transfers between devices with their start and end apart: 14 -> 14, of which waited for: 5 -> 4; matrix products, arithmetic and copies ran while one was open for 36% -> 41% of each run, Pallas kernels for 0% -> 0%
where the time goes in v2:
time: 226 us; the launch traced here: 223 us
  starting transfers between devices  65 us (29%)
  local copies, waits for them, and re-layouts  59.4 us (26%)
  other arithmetic  32.1 us (14%)
  matrix products  31.8 us (14%)
  waiting for transfers between devices  25.9 us (11%)
  blocking collectives  7.74 us (3%)
    all_to_all x2, starting transfers between devices, gather_blocks(): got = lax.all_to_all(spread, axis, 0, 0, tiled=True)  21.4 us
    all_to_all x2, waiting for transfers between devices, gather_blocks(): got = lax.all_to_all(spread, axis, 0, 0, tiled=True)  15.7 us
    ppermute x9, starting transfers between devices, passed_along(): lax.ppermute(shard, axis, [(i, (i + by) % length) for i in range(length)])  14.2 us
    all_to_all x1, starting transfers between devices, gather_stack(): return lax.all_to_all(spread, axis, 0, 0, tiled=True)  14 us
    all_to_all x1, starting transfers between devices, sum_to_owners(): got = lax.all_to_all(flat, axis, 0, 0, tiled=True)  12.2 us
    dot_general x1, matrix products, prior_values(): return jnp.dot(features, prior_weight, precision=lax.Precision.HIGHEST)  10.1 us
    unnamed x106, local copies, waits for them, and re-layouts  7.97 us
    psum x1, blocking collectives, shards(): summed = lax.psum(squares_local, 'path')  7.74 us
  transfers between devices with their start and end apart: 14, of which 4 were waited for; matrix products, arithmetic and copies ran while one was open for 41% of the time, Pallas kernels for 0%

profile of v2, /device:TPU:1, one launch (start us, length us, event | category | flops | bytes accessed | tf_op | source)
XLA Modules:
  0.0 223.5 jit_solution(6065780602359401756)
XLA Ops:
  3.1 2.5 %collective-permute-start = (f32[1024,32]{0,1:T(8,128)S(1)}, f32[1024,32]{0,1:T(8,128)}, u32[]{:S(2)}, u32[]{:S(2)}) collective-permute-start(f32[1024,32]{0,1:T(8,128)S(1)} %get-tuple-element.47), channel_id=1, source_target_pairs={{0,1},{1,2},{2,3},{3,0},{4,5},{5,6},{6,7},{7,4},{8,9},{9,10},{10,1... | collective-permute-start | bytes 393224 | tf_op jit(solution)/shard_map/ppermute | solution.py:17
  5.5 3.0 %collective-permute-start.1 = (f32[1024,32]{0,1:T(8,128)S(1)}, f32[1024,32]{0,1:T(8,128)}, u32[]{:S(2)}, u32[]{:S(2)}) collective-permute-start(f32[1024,32]{0,1:T(8,128)S(1)} %get-tuple-element.47), channel_id=1, source_target_pairs={{0,2},{1,3},{2,0},{3,1},{4,6},{5,7},{6,4},{7,5},{8,10},{9,11},{10,... | collective-permute-start | bytes 393224 | tf_op jit(solution)/shard_map/ppermute | solution.py:17
  14.2 14.0 %all-to-all-start = ((bf16[64,18,512]{2,1,0:T(8,128)(2,1)}), bf16[64,18,512]{2,1,0:T(8,128)(2,1)S(1)}, u32[]{:S(2)}, u32[]{:S(2)}) async-start(bf16[64,18,512]{2,1,0:T(8,128)(2,1)} %broadcast_in_dim.57), calls=%async_computation | async-start | bytes 3145728 | tf_op jit(solution)/shard_map/all_to_all | solution.py:58
  36.5 10.1 %fusion.24 = f32[512,16]{0,1:T(8,128)} fusion(f32[1024,16]{0,1:T(8,128)S(1)} %copy-done.14, f32[512,1024]{1,0:T(8,128)S(1)} %fusion.122, f32[1024]{0:T(1024)S(1)} %copy-done.33), kind=kOutput, calls=%fused_computation.41 | convolution fusion | flops 102236160 | bytes 2199552 | tf_op jit(solution)/shard_map/dot_general | solution.py:44
  80.5 2.4 %collective-permute-start.5 = (f32[3,24,384]{2,1,0:T(8,128)}, f32[3,24,384]{2,1,0:T(8,128)}, u32[]{:S(2)}, u32[]{:S(2)}) collective-permute-start(f32[3,24,384]{2,1,0:T(8,128)} %get-tuple-element.46), channel_id=1, source_target_pairs={{0,3},{1,0},{2,1},{3,2},{4,7},{5,4},{6,5},{7,6},{8,11},{9,8},{10,9... | collective-permute-start | bytes 331784 | tf_op jit(solution)/shard_map/ppermute | solution.py:17
  83.1 2.7 %fusion = f32[1152,1024]{1,0:T(8,128)S(1)} fusion(bf16[1152,512]{1,0:T(8,128)(2,1)} %reshape.329, bf16[1024,512]{1,0:T(8,128)(2,1)S(1)} %copy-done.2, f32[1024]{0:T(1024)S(1)} %copy-done.35, f32[1152]{0:T(1024)S(1)} %add.297), kind=kOutput, calls=%fused_computation.14 | convolution fusion | flops 1211498496 | bytes 6955520 | tf_op jit(solution)/shard_map/dot_general | solution.py:26
  85.8 3.1 %fusion.1 = f32[1152,128]{1,0:T(8,128)} fusion(f32[1024,128]{0,1:T(8,128)S(1)} %bitcast.104, f32[1152,1024]{1,0:T(8,128)S(1)} %fusion), kind=kOutput, calls=%fused_computation.15 | convolution fusion | flops 909508608 | bytes 5832704 | tf_op jit(solution)/shard_map/dot_general | solution.py:35
  88.9 12.2 %all-to-all-start.1 = ((f32[64,1,2304]{2,1,0:T(1,128)}), f32[64,1,2304]{2,1,0:T(1,128)}, u32[]{:S(2)}, u32[]{:S(2)}) async-start(f32[64,1,2304]{2,1,0:T(1,128)} %bitcast.103), calls=%async_computation.1 | async-start | bytes 1179648 | tf_op jit(solution)/shard_map/all_to_all | solution.py:72
  104.7 2.5 %gather_fusion.5 = f32[4,3,24,384]{3,2,1,0:T(8,128)} fusion(f32[4,3,24,384]{3,2,1,0:T(8,128)} %pad_maximum_fusion.1, s32[1024]{0:T(1024)} %copy-done.26), kind=kCustom, calls=%fused_computation.5 | custom fusion | bytes 884752 | tf_op jit(solution)/shard_map/jit(_take)/gather | solution.py:66
  107.2 3.4 %copy.110 = f32[4,3,24,384]{2,0,3,1:T(4,128)} copy(f32[4,3,24,384]{3,2,1,0:T(8,128)} %gather_fusion.5) | data formatting | bytes 884736 | tf_op jit(solution)/shard_map/jit(_take)/gather | solution.py:66
  110.6 2.3 %select_bitcast_fusion = f32[3,24,64,4,6]{1,3,4,2,0:T(4,128)S(1)} fusion(f32[4,3,24,64,6]{2,0,4,3,1:T(4,128)} %bitcast.102, pred[4]{0:T(512)(128)(4,1)S(1)} %copy-done.40), kind=kLoop, calls=%fused_computation.21 | loop fusion | flops 110592 | bytes 884740 | tf_op jit(solution)/shard_map/transpose | solution.py:135
  117.8 2.3 %copy.111 = f32[1,24,64,4,6]{1,4,3,2,0:T(8,128)} copy(f32[1,24,64,4,6]{1,3,4,2,0:T(4,128)} %get-tuple-element.38) | data formatting | bytes 294912 | tf_op jit(solution)/shard_map/slice | solution.py:137
  122.2 2.3 %copy.122 = f32[1,24,64,4,6]{1,4,3,2,0:T(8,128)} copy(f32[1,24,64,4,6]{1,3,4,2,0:T(4,128)} %get-tuple-element.36) | data formatting | bytes 294912 | tf_op jit(solution)/shard_map/slice | solution.py:137
  124.5 2.2 squeeze.44
  132.1 3.3 %all-to-all-start.2 = ((f32[4,1,576]{2,1,0:T(1,128)}), f32[4,1,576]{2,1,0:T(1,128)S(1)}, u32[]{:S(2)}, u32[]{:S(2)}) async-start(f32[4,1,576]{2,1,0:T(1,128)} %reshape.442), calls=%async_computation.2 | async-start | bytes 20480 | tf_op jit(solution)/shard_map/all_to_all | solution.py:124
  136.3 3.5 %all-to-all-done.2 = f32[4,1,576]{2,1,0:T(1,128)S(1)} async-done(((f32[4,1,576]{2,1,0:T(1,128)}), f32[4,1,576]{2,1,0:T(1,128)S(1)}, u32[]{:S(2)}, u32[]{:S(2)}) %all-to-all-start.2) | async-done | bytes 9248 | tf_op jit(solution)/shard_map/all_to_all | solution.py:124
  142.9 14.0 %all-to-all-start.3 = ((f32[64,1,384]{2,1,0:T(1,128)}), f32[64,1,384]{2,1,0:T(1,128)S(1)}, u32[]{:S(2)}, u32[]{:S(2)}) async-start(f32[64,1,384]{2,1,0:T(1,128)} %broadcast_in_dim.107), calls=%async_computation.3 | async-start | bytes 196608 | tf_op jit(solution)/shard_map/all_to_all | solution.py:51
  158.3 2.5 %scatter_fusion = f32[1024,16]{1,0:T(8,128)} fusion(f32[1024,16]{1,0:T(8,128)} %copy.105, s32[24]{0:T(128)S(1)} %copy-done.31, f32[24,16]{1,0:T(8,128)S(1)} %copy.106), kind=kCustom, calls=%fused_computation.10 | custom fusion | flops 384 | bytes 4704 | tf_op jit(solution)/shard_map/scatter-add | solution.py:166
  163.7 5.5 %all-to-all-done.3 = f32[64,1,384]{2,1,0:T(1,128)S(1)} async-done(((f32[64,1,384]{2,1,0:T(1,128)}), f32[64,1,384]{2,1,0:T(1,128)S(1)}, u32[]{:S(2)}, u32[]{:S(2)}) %all-to-all-start.3) | async-done | bytes 98336 | tf_op jit(solution)/shard_map/all_to_all | solution.py:51
  171.3 2.5 %scatter_fusion.1 = f32[1024,16]{1,0:T(8,128)} fusion(f32[1024,16]{1,0:T(8,128)} %get-tuple-element.43, s32[24]{0:T(128)S(1)} %copy-done.29, f32[24,16]{1,0:T(8,128)S(1)} %copy.118), kind=kCustom, calls=%fused_computation.11 | custom fusion | flops 384 | bytes 4704 | tf_op jit(solution)/shard_map/scatter-add | solution.py:166
  179.0 7.4 %all-to-all-start.4 = ((f32[64,1,384]{2,1,0:T(1,128)}), f32[64,1,384]{2,1,0:T(1,128)S(1)}, u32[]{:S(2)}, u32[]{:S(2)}) async-start(f32[64,1,384]{2,1,0:T(1,128)} %broadcast_in_dim.110), calls=%async_computation.4 | async-start | bytes 196608 | tf_op jit(solution)/shard_map/all_to_all | solution.py:51
  188.4 10.2 %all-to-all-done.4 = f32[64,1,384]{2,1,0:T(1,128)S(1)} async-done(((f32[64,1,384]{2,1,0:T(1,128)}), f32[64,1,384]{2,1,0:T(1,128)S(1)}, u32[]{:S(2)}, u32[]{:S(2)}) %all-to-all-start.4) | async-done | bytes 98336 | tf_op jit(solution)/shard_map/all_to_all | solution.py:51
  207.8 6.7 %collective-permute-done.6 = f32[512,16]{0,1:T(8,128)S(1)} collective-permute-done((f32[512,16]{0,1:T(8,128)S(1)}, f32[512,16]{0,1:T(8,128)S(1)}, u32[]{:S(2)}, u32[]{:S(2)}) %collective-permute-start.6) | collective-permute-done | bytes 32800 | tf_op jit(solution)/shard_map/ppermute | solution.py:17
  215.1 7.7 %psum.7 = f32[512]{0:T(512)S(1)} all-reduce(f32[512]{0:T(512)S(1)} %get-tuple-element.32), channel_id=1, replica_groups=mesh['blk'=64,'path'=4] {'path'}, use_global_device_ids=true, to_apply=%region_14.15 | all-reduce | flops 512 | bytes 4096 | tf_op jit(solution)/shard_map/psum | solution.py:187
  (231 shorter events, 93.9 us)
Async XLA Ops:
  0.6 35.1 %copy-start = (bf16[512,1024]{1,0:T(8,128)(2,1)S(1)}, bf16[512,1024]{1,0:T(8,128)(2,1)}, u32[]{:S(2)}) copy-start(bf16[512,1024]{1,0:T(8,128)(2,1)} %param.17) | copy-start | bytes 3145732
  3.1 62.4 %copy-start.10 = (f32[1024,32]{0,1:T(8,128)}, f32[1024,32]{0,1:T(8,128)S(1)}, u32[]{:S(2)}) copy-start(f32[1024,32]{0,1:T(8,128)S(1)} %get-tuple-element.47) | copy-start | bytes 393220
  3.1 62.4 %collective-permute-start = (f32[1024,32]{0,1:T(8,128)S(1)}, f32[1024,32]{0,1:T(8,128)}, u32[]{:S(2)}, u32[]{:S(2)}) collective-permute-start(f32[1024,32]{0,1:T(8,128)S(1)} %get-tuple-element.47), channel_id=1, source_target_pairs={{0,1},{1,2},{2,3},{3,0},{4,5},{5,6},{6,7},{7,4},{8,9},{9,10},{10,1... | collective-permute-start | bytes 393224 | tf_op jit(solution)/shard_map/ppermute | solution.py:17
  5.5 59.9 %collective-permute-start.1 = (f32[1024,32]{0,1:T(8,128)S(1)}, f32[1024,32]{0,1:T(8,128)}, u32[]{:S(2)}, u32[]{:S(2)}) collective-permute-start(f32[1024,32]{0,1:T(8,128)S(1)} %get-tuple-element.47), channel_id=1, source_target_pairs={{0,2},{1,3},{2,0},{3,1},{4,6},{5,7},{6,4},{7,5},{8,10},{9,11},{10,... | collective-permute-start | bytes 393224 | tf_op jit(solution)/shard_map/ppermute | solution.py:17
  8.5 56.9 %collective-permute-start.2 = (f32[1024,32]{0,1:T(8,128)S(1)}, f32[1024,32]{0,1:T(8,128)}, u32[]{:S(2)}, u32[]{:S(2)}) collective-permute-start(f32[1024,32]{0,1:T(8,128)S(1)} %get-tuple-element.47), channel_id=1, source_target_pairs={{0,3},{1,0},{2,1},{3,2},{4,7},{5,4},{6,5},{7,6},{8,11},{9,8},{10,9... | collective-permute-start | bytes 393224 | tf_op jit(solution)/shard_map/ppermute | solution.py:17
  14.2 54.9 %all-to-all-start = ((bf16[64,18,512]{2,1,0:T(8,128)(2,1)}), bf16[64,18,512]{2,1,0:T(8,128)(2,1)S(1)}, u32[]{:S(2)}, u32[]{:S(2)}) async-start(bf16[64,18,512]{2,1,0:T(8,128)(2,1)} %broadcast_in_dim.57), calls=%async_computation | async-start | bytes 3145728 | tf_op jit(solution)/shard_map/all_to_all | solution.py:58
  28.2 39.7 %copy-start.39 = (pred[4]{0:T(512)(128)(4,1)}, pred[4]{0:T(512)(128)(4,1)S(1)}, u32[]{:S(2)}) copy-start(pred[4]{0:T(512)(128)(4,1)S(1)} %compare_and_fusion) | copy-start | bytes 16
  28.3 38.2 %copy-start.26 = (s32[1024]{0:T(1024)}, s32[1024]{0:T(1024)S(1)}, u32[]{:S(2)}) copy-start(s32[1024]{0:T(1024)S(1)} %pad_clamp_fusion.4) | copy-start | bytes 12292
  32.1 30.5 %copy-start.24 = (s32[1024]{0:T(1024)}, s32[1024]{0:T(1024)S(1)}, u32[]{:S(2)}) copy-start(s32[1024]{0:T(1024)S(1)} %get-tuple-element.63) | copy-start | bytes 12292
  77.7 25.1 %collective-permute-start.3 = (f32[3,24,384]{2,1,0:T(8,128)}, f32[3,24,384]{2,1,0:T(8,128)}, u32[]{:S(2)}, u32[]{:S(2)}) collective-permute-start(f32[3,24,384]{2,1,0:T(8,128)} %get-tuple-element.46), channel_id=1, source_target_pairs={{0,1},{1,2},{2,3},{3,0},{4,5},{5,6},{6,7},{7,4},{8,9},{9,10},{10,1... | collective-permute-start | bytes 331784 | tf_op jit(solution)/shard_map/ppermute | solution.py:17
  79.2 23.6 %collective-permute-start.4 = (f32[3,24,384]{2,1,0:T(8,128)}, f32[3,24,384]{2,1,0:T(8,128)}, u32[]{:S(2)}, u32[]{:S(2)}) collective-permute-start(f32[3,24,384]{2,1,0:T(8,128)} %get-tuple-element.46), channel_id=1, source_target_pairs={{0,2},{1,3},{2,0},{3,1},{4,6},{5,7},{6,4},{7,5},{8,10},{9,11},{10,... | collective-permute-start | bytes 331784 | tf_op jit(solution)/shard_map/ppermute | solution.py:17
  80.5 22.3 %collective-permute-start.5 = (f32[3,24,384]{2,1,0:T(8,128)}, f32[3,24,384]{2,1,0:T(8,128)}, u32[]{:S(2)}, u32[]{:S(2)}) collective-permute-start(f32[3,24,384]{2,1,0:T(8,128)} %get-tuple-element.46), channel_id=1, source_target_pairs={{0,3},{1,0},{2,1},{3,2},{4,7},{5,4},{6,5},{7,6},{8,11},{9,8},{10,9... | collective-permute-start | bytes 331784 | tf_op jit(solution)/shard_map/ppermute | solution.py:17
  88.9 40.9 %all-to-all-start.1 = ((f32[64,1,2304]{2,1,0:T(1,128)}), f32[64,1,2304]{2,1,0:T(1,128)}, u32[]{:S(2)}, u32[]{:S(2)}) async-start(f32[64,1,2304]{2,1,0:T(1,128)} %bitcast.103), calls=%async_computation.1 | async-start | bytes 1179648 | tf_op jit(solution)/shard_map/all_to_all | solution.py:72
  101.1 25.6 %collective-permute-start.7 = (bf16[512,512]{1,0:T(8,128)(2,1)S(1)}, bf16[512,512]{1,0:T(8,128)(2,1)S(1)}, u32[]{:S(2)}, u32[]{:S(2)}) collective-permute-start(bf16[512,512]{1,0:T(8,128)(2,1)S(1)} %copy-done.4), channel_id=1, source_target_pairs={{0,4},{4,8},{8,12},{12,16},{16,20},{20,24},{24,28},{28,32},{32,36}... | collective-permute-start | bytes 1572872 | tf_op jit(solution)/shard_map/ppermute | solution.py:17
  129.8 28.5 %copy-start.31 = (s32[24]{0:T(128)S(1)}, s32[24]{0:T(128)}, u32[]{:S(2)}) copy-start(s32[24]{0:T(128)} %copy-done.30) | copy-start | bytes 292
  129.8 31.0 %copy-start.8 = (f32[1024,16]{1,0:T(8,128)S(1)}, f32[1024,16]{1,0:T(8,128)}, u32[]{:S(2)}) copy-start(f32[1024,16]{1,0:T(8,128)} %copy-done.7) | copy-start | bytes 196612
  132.1 7.7 %all-to-all-start.2 = ((f32[4,1,576]{2,1,0:T(1,128)}), f32[4,1,576]{2,1,0:T(1,128)S(1)}, u32[]{:S(2)}, u32[]{:S(2)}) async-start(f32[4,1,576]{2,1,0:T(1,128)} %reshape.442), calls=%async_computation.2 | async-start | bytes 20480 | tf_op jit(solution)/shard_map/all_to_all | solution.py:124
  141.1 28.6 %copy-start.6 = (f32[24,1536]{0,1:T(8,128)S(1)}, f32[24,1536]{0,1:T(8,128)}, u32[]{:S(2)}) copy-start(f32[24,1536]{0,1:T(8,128)} %squeeze.40) | copy-start | bytes 442372
  141.1 28.6 %copy-start.17 = (f32[24,16]{0,1:T(8,128)S(1)}, f32[24,16]{0,1:T(8,128)}, u32[]{:S(2)}) copy-start(f32[24,16]{0,1:T(8,128)} %copy.117) | copy-start | bytes 4612
  141.1 28.6 %copy-start.46 = (pred[24]{0:T(512)(128)(4,1)S(1)}, pred[24]{0:T(512)(128)(4,1)}, u32[]{:S(2)}) copy-start(pred[24]{0:T(512)(128)(4,1)} %iota_compare_fusion.1) | copy-start | bytes 76
  142.9 26.3 %all-to-all-start.3 = ((f32[64,1,384]{2,1,0:T(1,128)}), f32[64,1,384]{2,1,0:T(1,128)S(1)}, u32[]{:S(2)}, u32[]{:S(2)}) async-start(f32[64,1,384]{2,1,0:T(1,128)} %broadcast_in_dim.107), calls=%async_computation.3 | async-start | bytes 196608 | tf_op jit(solution)/shard_map/all_to_all | solution.py:51
  179.0 19.6 %all-to-all-start.4 = ((f32[64,1,384]{2,1,0:T(1,128)}), f32[64,1,384]{2,1,0:T(1,128)S(1)}, u32[]{:S(2)}, u32[]{:S(2)}) async-start(f32[64,1,384]{2,1,0:T(1,128)} %broadcast_in_dim.110), calls=%async_computation.4 | async-start | bytes 196608 | tf_op jit(solution)/shard_map/all_to_all | solution.py:51
  201.8 6.0 %collective-permute-start.8 = (f32[512,16]{0,1:T(8,128)S(1)}, f32[512,16]{0,1:T(8,128)S(1)}, u32[]{:S(2)}, u32[]{:S(2)}) collective-permute-start(f32[512,16]{0,1:T(8,128)S(1)} %fusion.53), channel_id=1, source_target_pairs={{0,4},{4,8},{8,12},{12,16},{16,20},{20,24},{24,28},{28,32},{32,36}... | collective-permute-start | bytes 98312 | tf_op jit(solution)/shard_map/ppermute | solution.py:17
  203.5 11.0 %collective-permute-start.6 = (f32[512,16]{0,1:T(8,128)S(1)}, f32[512,16]{0,1:T(8,128)S(1)}, u32[]{:S(2)}, u32[]{:S(2)}) collective-permute-start(f32[512,16]{0,1:T(8,128)S(1)} %fusion.55), channel_id=1, source_target_pairs={{0,8},{4,12},{8,16},{12,20},{16,24},{20,28},{24,32},{28,36},{32,40... | collective-permute-start | bytes 98312 | tf_op jit(solution)/shard_map/ppermute | solution.py:17
  (37 other events, 466.8 us)

commit v3 on v2

--- a/solution.py
+++ b/solution.py
@@ -139,11 +139,8 @@
     a_weight, b_weight = velocity_weights(steps + 1)
     own_rows_norms = square_norms(own_rows)
     cand_norms = square_norms(candidates)
-    neighbour_norms = square_norms(neighbour)
     own_start = kernel_apply(candidates, cand_norms, records, work_norms, start_weights)
-    next_start = kernel_apply(neighbour, neighbour_norms, records, work_norms, start_weights)
     own_slots = kernel_tile_of(candidates, cand_norms, own_rows, own_rows_norms)
-    next_slots = kernel_tile_of(neighbour, neighbour_norms, own_rows, own_rows_norms)
     weighted_updates = []
     updates = []
     for repeat in range(steps):
@@ -166,8 +163,15 @@
         velocity = (MOMENTUM * velocity).at[local_rows].add(step_update)
         coefficients = coefficients + velocity
         weighted_updates.append(b_weight[steps][repeat] * step_update)
+        if repeat == steps - 2:
+            last_exchanged = step_update
         if repeat < steps - 1:
             updates.append(gather_blocks(step_update, "blk").reshape(n_blk * slot_count, paths))
+
+    neighbour, _ = lax.optimization_barrier((neighbour, last_exchanged))
+    neighbour_norms = square_norms(neighbour)
+    next_start = kernel_apply(neighbour, neighbour_norms, records, work_norms, start_weights)
+    next_slots = kernel_tile_of(neighbour, neighbour_norms, own_rows, own_rows_norms)
 
     slot_weights = jnp.concatenate(weighted_updates, axis=0)
     own_sum = (

time: 226 us -> 236 us (1.044)
  local copies, waits for them, and re-layouts: 59.4 us -> 44.9 us
  starting transfers between devices: 65 us -> 75.8 us
  matrix products: 31.8 us -> 41.2 us
  waiting for transfers between devices: 25.9 us -> 30.3 us
    ppermute x9, waiting for transfers between devices: 6.73 us -> 18 us  [passed_along(): lax.ppermute(shard, axis, [(i, (i + by) % length) for i in range(length)])]
    all_to_all x2, starting transfers between devices: 21.4 us -> 28.8 us  [gather_blocks(): got = lax.all_to_all(spread, axis, 0, 0, tiled=True)]
    dot_general x8, matrix products: 6.79 us -> 12.9 us  [kernel_tile_of(): lax.dot_general(left_rows, right_rows, (((1,), (1,)), ((), ())), preferre...]
    slice x4, local copies, waits for them, and re-layouts: 7.28 us -> 3.23 us  [shards(): tile_of = {pair: tiles[k] for k, pair in enumerate(pairs)}]
    squeeze x3, local copies, waits for them, and re-layouts: 6.6 us -> 2.93 us  [shards(): tile_of = {pair: tiles[k] for k, pair in enumerate(pairs)}]
    all_to_all x1, waiting for transfers between devices: 3.46 us -> 0.01 us  [shards(): got = lax.all_to_all(share_sums, 'path', 0, 0, tiled=True)]
    all_to_all x2, waiting for transfers between devices: 15.7 us -> 12.3 us  [gather_blocks(): got = lax.all_to_all(spread, axis, 0, 0, tiled=True)]
    all_to_all x1, starting transfers between devices: 3.25 us -> 6.27 us  [shards(): got = lax.all_to_all(share_sums, 'path', 0, 0, tiled=True)]
  transfers between devices with their start and end apart: 14 -> 14, of which waited for: 4 -> 5; matrix products, arithmetic and copies ran while one was open for 41% -> 39% of each run, Pallas kernels for 0% -> 0%
where the time goes in v3:
time: 236 us; the launch traced here: 234 us
  starting transfers between devices  75.8 us (32%)
  local copies, waits for them, and re-layouts  44.9 us (19%)
  matrix products  41.2 us (17%)
  other arithmetic  31.2 us (13%)
  waiting for transfers between devices  30.3 us (13%)
  blocking collectives  9.68 us (4%)
    all_to_all x2, starting transfers between devices, gather_blocks(): got = lax.all_to_all(spread, axis, 0, 0, tiled=True)  28.8 us
    ppermute x9, waiting for transfers between devices, passed_along(): lax.ppermute(shard, axis, [(i, (i + by) % length) for i in range(length)])  18 us
    all_to_all x1, starting transfers between devices, gather_stack(): return lax.all_to_all(spread, axis, 0, 0, tiled=True)  13.8 us
    ppermute x9, starting transfers between devices, passed_along(): lax.ppermute(shard, axis, [(i, (i + by) % length) for i in range(length)])  13.8 us
    all_to_all x1, starting transfers between devices, sum_to_owners(): got = lax.all_to_all(flat, axis, 0, 0, tiled=True)  13.1 us
    dot_general x8, matrix products, kernel_tile_of(): lax.dot_general(left_rows, right_rows, (((1,), (1,)), ((), ())), preferre...  12.9 us
    all_to_all x2, waiting for transfers between devices, gather_blocks(): got = lax.all_to_all(spread, axis, 0, 0, tiled=True)  12.3 us
    dot_general x1, matrix products, prior_values(): return jnp.dot(features, prior_weight, precision=lax.Precision.HIGHEST)  10.1 us
  transfers between devices with their start and end apart: 14, of which 5 were waited for; matrix products, arithmetic and copies ran while one was open for 39% of the time, Pallas kernels for 0%

profile of v3, /device:TPU:1, one launch (start us, length us, event | category | flops | bytes accessed | tf_op | source)
XLA Modules:
  0.0 234.4 jit_solution(6460158237290680540)
XLA Ops:
  2.4 2.5 %collective-permute-start = (f32[1024,32]{0,1:T(8,128)S(1)}, f32[1024,32]{0,1:T(8,128)}, u32[]{:S(2)}, u32[]{:S(2)}) collective-permute-start(f32[1024,32]{0,1:T(8,128)S(1)} %get-tuple-element.49), channel_id=1, source_target_pairs={{0,1},{1,2},{2,3},{3,0},{4,5},{5,6},{6,7},{7,4},{8,9},{9,10},{10,1... | collective-permute-start | bytes 393224 | tf_op jit(solution)/shard_map/ppermute | solution.py:17
  5.0 3.0 %collective-permute-start.1 = (f32[1024,32]{0,1:T(8,128)S(1)}, f32[1024,32]{0,1:T(8,128)}, u32[]{:S(2)}, u32[]{:S(2)}) collective-permute-start(f32[1024,32]{0,1:T(8,128)S(1)} %get-tuple-element.49), channel_id=1, source_target_pairs={{0,2},{1,3},{2,0},{3,1},{4,6},{5,7},{6,4},{7,5},{8,10},{9,11},{10,... | collective-permute-start | bytes 393224 | tf_op jit(solution)/shard_map/ppermute | solution.py:17
  14.2 13.8 %all-to-all-start = ((bf16[64,18,512]{2,1,0:T(8,128)(2,1)}), bf16[64,18,512]{2,1,0:T(8,128)(2,1)S(1)}, u32[]{:S(2)}, u32[]{:S(2)}) async-start(bf16[64,18,512]{2,1,0:T(8,128)(2,1)} %broadcast_in_dim.57), calls=%async_computation | async-start | bytes 3145728 | tf_op jit(solution)/shard_map/all_to_all | solution.py:58
  29.3 2.1 gather_fusion.4
  40.7 10.1 %fusion.24 = f32[512,16]{0,1:T(8,128)} fusion(f32[1024,16]{0,1:T(8,128)S(1)} %copy-done.15, f32[512,1024]{1,0:T(8,128)S(1)} %fusion.115, f32[1024]{0:T(1024)S(1)} %copy-done.27), kind=kOutput, calls=%fused_computation.41 | convolution fusion | flops 102236160 | bytes 2199552 | tf_op jit(solution)/shard_map/dot_general | solution.py:44
  74.1 3.0 %fusion = f32[1152,1024]{1,0:T(8,128)S(1)} fusion(bf16[1152,512]{1,0:T(8,128)(2,1)} %reshape.329, bf16[1024,512]{1,0:T(8,128)(2,1)} %param.10, f32[1024]{0:T(1024)S(1)} %copy-done.29, f32[1152]{0:T(1024)S(1)} %add.297), kind=kOutput, calls=%fused_computation.14 | convolution fusion | flops 1211498496 | bytes 6955520 | tf_op jit(solution)/shard_map/dot_general | solution.py:26
  77.1 3.2 %fusion.1 = f32[1152,128]{1,0:T(8,128)} fusion(f32[1024,128]{0,1:T(8,128)S(1)} %bitcast.104, f32[1152,1024]{1,0:T(8,128)S(1)} %fusion), kind=kOutput, calls=%fused_computation.15 | convolution fusion | flops 909508608 | bytes 5832704 | tf_op jit(solution)/shard_map/dot_general | solution.py:35
  80.3 13.1 %all-to-all-start.1 = ((f32[64,1,2304]{2,1,0:T(1,128)}), f32[64,1,2304]{2,1,0:T(1,128)}, u32[]{:S(2)}, u32[]{:S(2)}) async-start(f32[64,1,2304]{2,1,0:T(1,128)} %bitcast.11), calls=%async_computation.1 | async-start | bytes 1179648 | tf_op jit(solution)/shard_map/all_to_all | solution.py:72
  97.8 2.3 collective-permute-start.5
  101.2 2.5 %collective-permute-start.7 = (bf16[512,512]{1,0:T(8,128)(2,1)}, bf16[512,512]{1,0:T(8,128)(2,1)}, u32[]{:S(2)}, u32[]{:S(2)}) collective-permute-start(bf16[512,512]{1,0:T(8,128)(2,1)} %param.16), channel_id=1, source_target_pairs={{0,4},{4,8},{8,12},{12,16},{16,20},{20,24},{24,28},{28,32},{32,36}... | collective-permute-start | bytes 1572872 | tf_op jit(solution)/shard_map/ppermute | solution.py:17
  104.4 10.2 %collective-permute-done.4 = f32[3,24,384]{2,1,0:T(8,128)S(1)} collective-permute-done((f32[3,24,384]{2,1,0:T(8,128)S(1)}, f32[3,24,384]{2,1,0:T(8,128)S(1)}, u32[]{:S(2)}, u32[]{:S(2)}) %collective-permute-start.4) | collective-permute-done | bytes 110624 | tf_op jit(solution)/shard_map/ppermute | solution.py:17
  115.4 2.4 %copy.110 = f32[4,3,24,384]{2,0,3,1:T(4,128)} copy(f32[4,3,24,384]{3,2,1,0:T(8,128)S(1)} %gather_fusion.5) | data formatting | bytes 884736 | tf_op jit(solution)/shard_map/jit(_take)/gather | solution.py:66
  117.7 2.3 select_bitcast_fusion
  123.6 6.3 %all-to-all-start.2 = ((f32[4,1,576]{2,1,0:T(1,128)}), f32[4,1,576]{2,1,0:T(1,128)S(1)}, u32[]{:S(2)}, u32[]{:S(2)}) async-start(f32[4,1,576]{2,1,0:T(1,128)} %reshape.442), calls=%async_computation.2 | async-start | bytes 20480 | tf_op jit(solution)/shard_map/all_to_all | solution.py:124
  139.3 22.9 %all-to-all-start.3 = ((f32[64,1,384]{2,1,0:T(1,128)}), f32[64,1,384]{2,1,0:T(1,128)S(1)}, u32[]{:S(2)}, u32[]{:S(2)}) async-start(f32[64,1,384]{2,1,0:T(1,128)} %broadcast_in_dim.107), calls=%async_computation.3 | async-start | bytes 196608 | tf_op jit(solution)/shard_map/all_to_all | solution.py:51
  162.3 2.5 %scatter_fusion = f32[1024,16]{1,0:T(8,128)} fusion(f32[1024,16]{1,0:T(8,128)} %copy.105, s32[24]{0:T(128)S(1)} %copy-done.26, f32[24,16]{1,0:T(8,128)S(1)} %copy.106), kind=kCustom, calls=%fused_computation.10 | custom fusion | flops 384 | bytes 4704 | tf_op jit(solution)/shard_map/scatter-add | solution.py:163
  168.4 6.9 %all-to-all-done.3 = f32[64,1,384]{2,1,0:T(1,128)S(1)} async-done(((f32[64,1,384]{2,1,0:T(1,128)}), f32[64,1,384]{2,1,0:T(1,128)S(1)}, u32[]{:S(2)}, u32[]{:S(2)}) %all-to-all-start.3) | async-done | bytes 98336 | tf_op jit(solution)/shard_map/all_to_all | solution.py:51
  177.8 3.2 %fusion.117 = f32[512,1024]{1,0:T(8,128)} fusion(bf16[512,512]{1,0:T(8,128)(2,1)} %collective-permute-done.7, bf16[1024,512]{1,0:T(8,128)(2,1)S(1)} %copy-done.2), kind=kOutput, calls=%fused_computation.199 | convolution fusion | flops 536870912 | bytes 3670016 | tf_op jit(solution)/shard_map/dot_general | solution.py:26
  182.4 2.5 %scatter_fusion.1 = f32[1024,16]{1,0:T(8,128)} fusion(f32[1024,16]{1,0:T(8,128)} %get-tuple-element.45, s32[24]{0:T(128)S(1)} %copy-done.24, f32[24,16]{1,0:T(8,128)S(1)} %copy.118), kind=kCustom, calls=%fused_computation.11 | custom fusion | flops 384 | bytes 4704 | tf_op jit(solution)/shard_map/scatter-add | solution.py:163
  188.2 5.9 %all-to-all-start.4 = ((f32[64,1,384]{2,1,0:T(1,128)}), f32[64,1,384]{2,1,0:T(1,128)S(1)}, u32[]{:S(2)}, u32[]{:S(2)}) async-start(f32[64,1,384]{2,1,0:T(1,128)} %broadcast_in_dim.110), calls=%async_computation.4 | async-start | bytes 196608 | tf_op jit(solution)/shard_map/all_to_all | solution.py:51
  194.2 3.7 %fusion.8 = f32[512,32]{0,1:T(8,128)} fusion(f32[1024,32]{0,1:T(8,128)} %copy-done.12, f32[512,1024]{1,0:T(8,128)} %fusion.117, f32[512]{0:T(512)S(1)} %multiply_reduce_fusion.2, f32[1024]{0:T(1024)S(1)} %copy-done.30), kind=kOutput, calls=%fused_computation.24 | convolution fusion | flops 103809024 | bytes 2299904 | tf_op jit(solution)/shard_map/dot_general | solution.py:35
  201.9 5.4 %all-to-all-done.4 = f32[64,1,384]{2,1,0:T(1,128)S(1)} async-done(((f32[64,1,384]{2,1,0:T(1,128)}), f32[64,1,384]{2,1,0:T(1,128)S(1)}, u32[]{:S(2)}, u32[]{:S(2)}) %all-to-all-start.4) | async-done | bytes 98336 | tf_op jit(solution)/shard_map/all_to_all | solution.py:51
  216.4 7.0 %collective-permute-done.6 = f32[512,16]{0,1:T(8,128)S(1)} collective-permute-done((f32[512,16]{0,1:T(8,128)S(1)}, f32[512,16]{0,1:T(8,128)S(1)}, u32[]{:S(2)}, u32[]{:S(2)}) %collective-permute-start.6) | collective-permute-done | bytes 32800 | tf_op jit(solution)/shard_map/ppermute | solution.py:17
  224.1 9.7 %psum.7 = f32[512]{0:T(512)S(1)} all-reduce(f32[512]{0:T(512)S(1)} %get-tuple-element.34), channel_id=1, replica_groups=mesh['blk'=64,'path'=4] {'path'}, use_global_device_ids=true, to_apply=%region_14.15 | all-reduce | flops 512 | bytes 4096 | tf_op jit(solution)/shard_map/psum | solution.py:191
  (211 shorter events, 86.7 us)
Async XLA Ops:
  0.6 38.2 %copy-start = (bf16[512,1024]{1,0:T(8,128)(2,1)S(1)}, bf16[512,1024]{1,0:T(8,128)(2,1)}, u32[]{:S(2)}) copy-start(bf16[512,1024]{1,0:T(8,128)(2,1)} %param.17) | copy-start | bytes 3145732
  2.4 64.9 %copy-start.12 = (f32[1024,32]{0,1:T(8,128)}, f32[1024,32]{0,1:T(8,128)S(1)}, u32[]{:S(2)}) copy-start(f32[1024,32]{0,1:T(8,128)S(1)} %get-tuple-element.49) | copy-start | bytes 393220
  2.4 64.9 %collective-permute-start = (f32[1024,32]{0,1:T(8,128)S(1)}, f32[1024,32]{0,1:T(8,128)}, u32[]{:S(2)}, u32[]{:S(2)}) collective-permute-start(f32[1024,32]{0,1:T(8,128)S(1)} %get-tuple-element.49), channel_id=1, source_target_pairs={{0,1},{1,2},{2,3},{3,0},{4,5},{5,6},{6,7},{7,4},{8,9},{9,10},{10,1... | collective-permute-start | bytes 393224 | tf_op jit(solution)/shard_map/ppermute | solution.py:17
  5.0 62.3 %collective-permute-start.1 = (f32[1024,32]{0,1:T(8,128)S(1)}, f32[1024,32]{0,1:T(8,128)}, u32[]{:S(2)}, u32[]{:S(2)}) collective-permute-start(f32[1024,32]{0,1:T(8,128)S(1)} %get-tuple-element.49), channel_id=1, source_target_pairs={{0,2},{1,3},{2,0},{3,1},{4,6},{5,7},{6,4},{7,5},{8,10},{9,11},{10,... | collective-permute-start | bytes 393224 | tf_op jit(solution)/shard_map/ppermute | solution.py:17
  8.0 59.4 %collective-permute-start.2 = (f32[1024,32]{0,1:T(8,128)S(1)}, f32[1024,32]{0,1:T(8,128)}, u32[]{:S(2)}, u32[]{:S(2)}) collective-permute-start(f32[1024,32]{0,1:T(8,128)S(1)} %get-tuple-element.49), channel_id=1, source_target_pairs={{0,3},{1,0},{2,1},{3,2},{4,7},{5,4},{6,5},{7,6},{8,11},{9,8},{10,9... | collective-permute-start | bytes 393224 | tf_op jit(solution)/shard_map/ppermute | solution.py:17
  9.5 23.9 %copy-start.22 = (s32[24]{0:T(128)}, s32[24]{0:T(128)S(1)}, u32[]{:S(2)}) copy-start(s32[24]{0:T(128)S(1)} %get-tuple-element.62) | copy-start | bytes 292
  9.5 23.9 %copy-start.23 = (s32[24]{0:T(128)}, s32[24]{0:T(128)S(1)}, u32[]{:S(2)}) copy-start(s32[24]{0:T(128)S(1)} %get-tuple-element.63) | copy-start | bytes 292
  12.9 16.4 %copy-start.36 = (s32[3,64]{1,0:T(4,128)S(1)}, s32[3,64]{1,0:T(4,128)}, u32[]{:S(2)}) copy-start(s32[3,64]{1,0:T(4,128)} %param.15) | copy-start | bytes 2308
  14.2 56.9 %all-to-all-start = ((bf16[64,18,512]{2,1,0:T(8,128)(2,1)}), bf16[64,18,512]{2,1,0:T(8,128)(2,1)S(1)}, u32[]{:S(2)}, u32[]{:S(2)}) async-start(bf16[64,18,512]{2,1,0:T(8,128)(2,1)} %broadcast_in_dim.57), calls=%async_computation | async-start | bytes 3145728 | tf_op jit(solution)/shard_map/all_to_all | solution.py:58
  33.4 30.4 %copy-start.21 = (s32[1024]{0:T(1024)}, s32[1024]{0:T(1024)S(1)}, u32[]{:S(2)}) copy-start(s32[1024]{0:T(1024)S(1)} %get-tuple-element.66) | copy-start | bytes 12292
  33.4 32.1 %copy-start.20 = (s32[1024]{0:T(1024)}, s32[1024]{0:T(1024)S(1)}, u32[]{:S(2)}) copy-start(s32[1024]{0:T(1024)S(1)} %get-tuple-element.65) | copy-start | bytes 12292
  36.7 15.9 %copy-start.28 = (f32[1024]{0:T(1024)}, f32[1024]{0:T(1024)S(1)}, u32[]{:S(2)}) copy-start(f32[1024]{0:T(1024)S(1)} %multiply_reduce_fusion.1) | copy-start | bytes 12292
  80.3 39.7 %all-to-all-start.1 = ((f32[64,1,2304]{2,1,0:T(1,128)}), f32[64,1,2304]{2,1,0:T(1,128)}, u32[]{:S(2)}, u32[]{:S(2)}) async-start(f32[64,1,2304]{2,1,0:T(1,128)} %bitcast.11), calls=%async_computation.1 | async-start | bytes 1179648 | tf_op jit(solution)/shard_map/all_to_all | solution.py:72
  96.3 8.2 %collective-permute-start.3 = (f32[3,24,384]{2,1,0:T(8,128)S(1)}, f32[3,24,384]{2,1,0:T(8,128)S(1)}, u32[]{:S(2)}, u32[]{:S(2)}) collective-permute-start(f32[3,24,384]{2,1,0:T(8,128)S(1)} %get-tuple-element.48), channel_id=1, source_target_pairs={{0,1},{1,2},{2,3},{3,0},{4,5},{5,6},{6,7},{7,4},{8,9},{9,10},{10,1... | collective-permute-start | bytes 331784 | tf_op jit(solution)/shard_map/ppermute | solution.py:17
  96.6 18.1 %collective-permute-start.4 = (f32[3,24,384]{2,1,0:T(8,128)S(1)}, f32[3,24,384]{2,1,0:T(8,128)S(1)}, u32[]{:S(2)}, u32[]{:S(2)}) collective-permute-start(f32[3,24,384]{2,1,0:T(8,128)S(1)} %get-tuple-element.48), channel_id=1, source_target_pairs={{0,2},{1,3},{2,0},{3,1},{4,6},{5,7},{6,4},{7,5},{8,10},{9,11},{10,... | collective-permute-start | bytes 331784 | tf_op jit(solution)/shard_map/ppermute | solution.py:17
  97.8 16.8 %collective-permute-start.5 = (f32[3,24,384]{2,1,0:T(8,128)S(1)}, f32[3,24,384]{2,1,0:T(8,128)S(1)}, u32[]{:S(2)}, u32[]{:S(2)}) collective-permute-start(f32[3,24,384]{2,1,0:T(8,128)S(1)} %get-tuple-element.48), channel_id=1, source_target_pairs={{0,3},{1,0},{2,1},{3,2},{4,7},{5,4},{6,5},{7,6},{8,11},{9,8},{10,9... | collective-permute-start | bytes 331784 | tf_op jit(solution)/shard_map/ppermute | solution.py:17
  101.2 76.6 %collective-permute-start.7 = (bf16[512,512]{1,0:T(8,128)(2,1)}, bf16[512,512]{1,0:T(8,128)(2,1)}, u32[]{:S(2)}, u32[]{:S(2)}) collective-permute-start(bf16[512,512]{1,0:T(8,128)(2,1)} %param.16), channel_id=1, source_target_pairs={{0,4},{4,8},{8,12},{12,16},{16,20},{20,24},{24,28},{28,32},{32,36}... | collective-permute-start | bytes 1572872 | tf_op jit(solution)/shard_map/ppermute | solution.py:17
  123.6 12.5 %all-to-all-start.2 = ((f32[4,1,576]{2,1,0:T(1,128)}), f32[4,1,576]{2,1,0:T(1,128)S(1)}, u32[]{:S(2)}, u32[]{:S(2)}) async-start(f32[4,1,576]{2,1,0:T(1,128)} %reshape.442), calls=%async_computation.2 | async-start | bytes 20480 | tf_op jit(solution)/shard_map/all_to_all | solution.py:124
  134.9 29.9 %copy-start.7 = (f32[1024,16]{1,0:T(8,128)S(1)}, f32[1024,16]{1,0:T(8,128)}, u32[]{:S(2)}) copy-start(f32[1024,16]{1,0:T(8,128)} %copy-done.6) | copy-start | bytes 196612
  135.1 27.2 %copy-start.26 = (s32[24]{0:T(128)S(1)}, s32[24]{0:T(128)}, u32[]{:S(2)}) copy-start(s32[24]{0:T(128)} %copy-done.25) | copy-start | bytes 292
  139.3 36.0 %all-to-all-start.3 = ((f32[64,1,384]{2,1,0:T(1,128)}), f32[64,1,384]{2,1,0:T(1,128)S(1)}, u32[]{:S(2)}, u32[]{:S(2)}) async-start(f32[64,1,384]{2,1,0:T(1,128)} %broadcast_in_dim.107), calls=%async_computation.3 | async-start | bytes 196608 | tf_op jit(solution)/shard_map/all_to_all | solution.py:51
  188.2 19.0 %all-to-all-start.4 = ((f32[64,1,384]{2,1,0:T(1,128)}), f32[64,1,384]{2,1,0:T(1,128)S(1)}, u32[]{:S(2)}, u32[]{:S(2)}) async-start(f32[64,1,384]{2,1,0:T(1,128)} %broadcast_in_dim.110), calls=%async_computation.4 | async-start | bytes 196608 | tf_op jit(solution)/shard_map/all_to_all | solution.py:51
  210.4 6.0 %collective-permute-start.8 = (f32[512,16]{0,1:T(8,128)S(1)}, f32[512,16]{0,1:T(8,128)S(1)}, u32[]{:S(2)}, u32[]{:S(2)}) collective-permute-start(f32[512,16]{0,1:T(8,128)S(1)} %fusion.58), channel_id=1, source_target_pairs={{0,4},{4,8},{8,12},{12,16},{16,20},{20,24},{24,28},{28,32},{32,36}... | collective-permute-start | bytes 98312 | tf_op jit(solution)/shard_map/ppermute | solution.py:17
  212.2 11.3 %collective-permute-start.6 = (f32[512,16]{0,1:T(8,128)S(1)}, f32[512,16]{0,1:T(8,128)S(1)}, u32[]{:S(2)}, u32[]{:S(2)}) collective-permute-start(f32[512,16]{0,1:T(8,128)S(1)} %fusion.60), channel_id=1, source_target_pairs={{0,8},{4,12},{8,16},{12,20},{16,24},{20,28},{24,32},{28,36},{32,40... | collective-permute-start | bytes 98312 | tf_op jit(solution)/shard_map/ppermute | solution.py:17
  (27 other events, 215.1 us)

commit v4 on v2

--- a/solution.py
+++ b/solution.py
@@ -132,10 +132,9 @@
         theirs = gathered[:, s * share:(s + 1) * share].reshape(n_blk * share, -1)
         tiles.append(kernel_tile_of(mine, square_norms(mine), theirs, square_norms(theirs)))
     tiles = gather_by_permutes(jnp.stack(tiles), "path")
-    tiles = tiles.reshape(n_path, len(pairs), slot_count, n_blk, share).transpose(1, 2, 3, 0, 4)
-    tiles = tiles.reshape(len(pairs), slot_count, n_blk * slot_count)
-    tile_of = {pair: tiles[k] for k, pair in enumerate(pairs)}
-
+    tile_of = {pair: tiles[:, k] for k, pair in enumerate(pairs)}
+
+    neighbour, _ = lax.optimization_barrier((neighbour, start_sums))
     a_weight, b_weight = velocity_weights(steps + 1)
     own_rows_norms = square_norms(own_rows)
     cand_norms = square_norms(candidates)
@@ -154,8 +153,11 @@
         if repeat > 0:
             total = total + a_weight[repeat] * start_sums[repeat, :, paths:]
         for earlier in range(repeat):
-            cross = jnp.dot(
-                tile_of[(repeat, earlier)], updates[earlier], precision=lax.Precision.HIGH
+            cross = lax.dot_general(
+                tile_of[(repeat, earlier)],
+                updates[earlier],
+                (((0, 2), (0, 1)), ((), ())),
+                precision=lax.Precision.HIGH,
             )
             total = total + b_weight[repeat][earlier] * cross
         product = total / root_count
@@ -167,7 +169,9 @@
         coefficients = coefficients + velocity
         weighted_updates.append(b_weight[steps][repeat] * step_update)
         if repeat < steps - 1:
-            updates.append(gather_blocks(step_update, "blk").reshape(n_blk * slot_count, paths))
+            every_update = gather_blocks(step_update, "blk").reshape(n_blk, n_path, share, paths)
+            every_update = every_update.transpose(1, 0, 2, 3).reshape(n_path, n_blk * share, paths)
+            updates.append(every_update)
 
     slot_weights = jnp.concatenate(weighted_updates, axis=0)
     own_sum = (

time: 226 us -> 224 us (level)
  local copies, waits for them, and re-layouts: 59.4 us -> 40.6 us
  starting transfers between devices: 65 us -> 76.5 us
  matrix products: 31.8 us -> 38.6 us
  other arithmetic: 32.1 us -> 26.8 us
  waiting for transfers between devices: 25.9 us -> 29.9 us
    all_to_all x2, starting transfers between devices: 21.4 us -> 32 us  [gather_blocks(): got = lax.all_to_all(spread, axis, 0, 0, tiled=True)]
    ppermute x9, waiting for transfers between devices: 6.73 us -> 17.2 us  [passed_along(): lax.ppermute(shard, axis, [(i, (i + by) % length) for i in range(length)])]
    slice x4 -> x0, local copies, waits for them, and re-layouts: 7.28 us -> none  [shards(): tile_of = {pair: tiles[k] for k, pair in enumerate(pairs)}]
    squeeze x3 -> x0, local copies, waits for them, and re-layouts: 6.6 us -> none  [shards(): tile_of = {pair: tiles[k] for k, pair in enumerate(pairs)}]
    all_to_all x2, waiting for transfers between devices: 15.7 us -> 9.15 us  [gather_blocks(): got = lax.all_to_all(spread, axis, 0, 0, tiled=True)]
    dot_general x8, matrix products: 6.79 us -> 13 us  [kernel_tile_of(): lax.dot_general(left_rows, right_rows, (((1,), (1,)), ((), ())), preferre...]
    gather x3 -> x2, local copies, waits for them, and re-layouts: 7.27 us -> 3.21 us  [gather_by_permutes(): return jnp.take(jnp.stack(moved), order, axis=0)]
    unnamed x106 -> x102, local copies, waits for them, and re-layouts: 7.97 us -> 6.25 us
  transfers between devices with their start and end apart: 14 -> 14, of which waited for: 4 -> 6; matrix products, arithmetic and copies ran while one was open for 41% -> 37% of each run, Pallas kernels for 0% -> 0%
where the time goes in v4:
time: 224 us; the launch traced here: 222 us
  starting transfers between devices  76.5 us (34%)
  local copies, waits for them, and re-layouts  40.6 us (18%)
  matrix products  38.6 us (17%)
  waiting for transfers between devices  29.9 us (13%)
  other arithmetic  26.8 us (12%)
  blocking collectives  7.75 us (3%)
    all_to_all x2, starting transfers between devices, gather_blocks(): got = lax.all_to_all(spread, axis, 0, 0, tiled=True)  32 us
    ppermute x9, waiting for transfers between devices, passed_along(): lax.ppermute(shard, axis, [(i, (i + by) % length) for i in range(length)])  17.2 us
    all_to_all x1, starting transfers between devices, gather_stack(): return lax.all_to_all(spread, axis, 0, 0, tiled=True)  14 us
    dot_general x8, matrix products, kernel_tile_of(): lax.dot_general(left_rows, right_rows, (((1,), (1,)), ((), ())), preferre...  13 us
    all_to_all x1, starting transfers between devices, sum_to_owners(): got = lax.all_to_all(flat, axis, 0, 0, tiled=True)  13 us
    ppermute x9, starting transfers between devices, passed_along(): lax.ppermute(shard, axis, [(i, (i + by) % length) for i in range(length)])  12.9 us
    dot_general x1, matrix products, prior_values(): return jnp.dot(features, prior_weight, precision=lax.Precision.HIGHEST)  10.1 us
    all_to_all x2, waiting for transfers between devices, gather_blocks(): got = lax.all_to_all(spread, axis, 0, 0, tiled=True)  9.15 us
  transfers between devices with their start and end apart: 14, of which 6 were waited for; matrix products, arithmetic and copies ran while one was open for 37% of the time, Pallas kernels for 0%

profile of v4, /device:TPU:1, one launch (start us, length us, event | category | flops | bytes accessed | tf_op | source)
XLA Modules:
  0.0 221.6 jit_solution(5413166869289213965)
XLA Ops:
  2.4 2.5 %collective-permute-start = (f32[1024,32]{0,1:T(8,128)S(1)}, f32[1024,32]{0,1:T(8,128)}, u32[]{:S(2)}, u32[]{:S(2)}) collective-permute-start(f32[1024,32]{0,1:T(8,128)S(1)} %get-tuple-element.46), channel_id=1, source_target_pairs={{0,1},{1,2},{2,3},{3,0},{4,5},{5,6},{6,7},{7,4},{8,9},{9,10},{10,1... | collective-permute-start | bytes 393224 | tf_op jit(solution)/shard_map/ppermute | solution.py:17
  5.0 3.0 %collective-permute-start.1 = (f32[1024,32]{0,1:T(8,128)S(1)}, f32[1024,32]{0,1:T(8,128)}, u32[]{:S(2)}, u32[]{:S(2)}) collective-permute-start(f32[1024,32]{0,1:T(8,128)S(1)} %get-tuple-element.46), channel_id=1, source_target_pairs={{0,2},{1,3},{2,0},{3,1},{4,6},{5,7},{6,4},{7,5},{8,10},{9,11},{10,... | collective-permute-start | bytes 393224 | tf_op jit(solution)/shard_map/ppermute | solution.py:17
  13.7 14.0 %all-to-all-start = ((bf16[64,18,512]{2,1,0:T(8,128)(2,1)}), bf16[64,18,512]{2,1,0:T(8,128)(2,1)S(1)}, u32[]{:S(2)}, u32[]{:S(2)}) async-start(bf16[64,18,512]{2,1,0:T(8,128)(2,1)} %broadcast_in_dim.57), calls=%async_computation | async-start | bytes 3145728 | tf_op jit(solution)/shard_map/all_to_all | solution.py:58
  28.9 2.1 gather_fusion.4
  37.6 10.1 %fusion.24 = f32[512,16]{0,1:T(8,128)} fusion(f32[1024,16]{0,1:T(8,128)S(1)} %copy-done.19, f32[512,1024]{1,0:T(8,128)S(1)} %fusion.118, f32[1024]{0:T(1024)S(1)} %copy-done.33), kind=kOutput, calls=%fused_computation.40 | convolution fusion | flops 102236160 | bytes 2199552 | tf_op jit(solution)/shard_map/dot_general | solution.py:44
  48.5 2.1 fusion.16
  70.9 3.1 %fusion = f32[1152,1024]{1,0:T(8,128)S(1)} fusion(bf16[1152,512]{1,0:T(8,128)(2,1)} %reshape.326, bf16[1024,512]{1,0:T(8,128)(2,1)} %param.10, f32[1024]{0:T(1024)S(1)} %copy-done.35, f32[1152]{0:T(1024)S(1)} %add.297), kind=kOutput, calls=%fused_computation.14 | convolution fusion | flops 1211498496 | bytes 6955520 | tf_op jit(solution)/shard_map/dot_general | solution.py:26
  74.0 3.1 %fusion.1 = f32[1152,128]{1,0:T(8,128)} fusion(f32[1024,128]{0,1:T(8,128)S(1)} %bitcast.144, f32[1152,1024]{1,0:T(8,128)S(1)} %fusion), kind=kOutput, calls=%fused_computation.15 | convolution fusion | flops 909508608 | bytes 5832704 | tf_op jit(solution)/shard_map/dot_general | solution.py:35
  77.1 13.0 %all-to-all-start.1 = ((f32[64,1,2304]{2,1,0:T(1,128)}), f32[64,1,2304]{2,1,0:T(1,128)}, u32[]{:S(2)}, u32[]{:S(2)}) async-start(f32[64,1,2304]{2,1,0:T(1,128)} %bitcast.143), calls=%async_computation.1 | async-start | bytes 1179648 | tf_op jit(solution)/shard_map/all_to_all | solution.py:72
  102.8 2.3 %collective-permute-start.5 = (f32[3,24,384]{2,1,0:T(8,128)S(1)}, f32[3,24,384]{2,1,0:T(8,128)S(1)}, u32[]{:S(2)}, u32[]{:S(2)}) collective-permute-start(f32[3,24,384]{2,1,0:T(8,128)S(1)} %get-tuple-element.45), channel_id=1, source_target_pairs={{0,3},{1,0},{2,1},{3,2},{4,7},{5,4},{6,5},{7,6},{8,11},{9,8},{10,9... | collective-permute-start | bytes 331784 | tf_op jit(solution)/shard_map/ppermute | solution.py:17
  106.3 4.8 %collective-permute-done.3 = f32[3,24,384]{2,1,0:T(8,128)S(1)} collective-permute-done((f32[3,24,384]{2,1,0:T(8,128)S(1)}, f32[3,24,384]{2,1,0:T(8,128)S(1)}, u32[]{:S(2)}, u32[]{:S(2)}) %collective-permute-start.3) | collective-permute-done | bytes 110624 | tf_op jit(solution)/shard_map/ppermute | solution.py:17
  111.1 4.7 %collective-permute-done.4 = f32[3,24,384]{2,1,0:T(8,128)S(1)} collective-permute-done((f32[3,24,384]{2,1,0:T(8,128)S(1)}, f32[3,24,384]{2,1,0:T(8,128)S(1)}, u32[]{:S(2)}, u32[]{:S(2)}) %collective-permute-start.4) | collective-permute-done | bytes 110624 | tf_op jit(solution)/shard_map/ppermute | solution.py:17
  120.5 4.6 %all-to-all-start.2 = ((f32[4,1,576]{2,1,0:T(1,128)}), f32[4,1,576]{2,1,0:T(1,128)S(1)}, u32[]{:S(2)}, u32[]{:S(2)}) async-start(f32[4,1,576]{2,1,0:T(1,128)} %reshape.442), calls=%async_computation.2 | async-start | bytes 20480 | tf_op jit(solution)/shard_map/all_to_all | solution.py:124
  126.0 3.6 %all-to-all-done.2 = f32[4,1,576]{2,1,0:T(1,128)S(1)} async-done(((f32[4,1,576]{2,1,0:T(1,128)}), f32[4,1,576]{2,1,0:T(1,128)S(1)}, u32[]{:S(2)}, u32[]{:S(2)}) %all-to-all-start.2) | async-done | bytes 9248 | tf_op jit(solution)/shard_map/all_to_all | solution.py:124
  132.2 3.2 %fusion.120 = f32[512,1024]{1,0:T(8,128)} fusion(bf16[512,512]{1,0:T(8,128)(2,1)} %collective-permute-done.7, bf16[1024,512]{1,0:T(8,128)(2,1)S(1)} %copy-done.2), kind=kOutput, calls=%fused_computation.205 | convolution fusion | flops 536870912 | bytes 3670016 | tf_op jit(solution)/shard_map/dot_general | solution.py:26
  136.6 21.3 %all-to-all-start.3 = ((f32[64,1,384]{2,1,0:T(1,128)}), f32[64,1,384]{2,1,0:T(1,128)S(1)}, u32[]{:S(2)}, u32[]{:S(2)}) async-start(f32[64,1,384]{2,1,0:T(1,128)} %broadcast_in_dim.107), calls=%async_computation.3 | async-start | bytes 196608 | tf_op jit(solution)/shard_map/all_to_all | solution.py:51
  162.2 3.7 %fusion.8 = f32[512,32]{0,1:T(8,128)} fusion(f32[1024,32]{0,1:T(8,128)S(1)} %copy-done.15, f32[512,1024]{1,0:T(8,128)} %fusion.120, f32[512]{0:T(512)S(1)} %multiply_reduce_fusion.2, f32[1024]{0:T(1024)S(1)} %copy-done.36), kind=kOutput, calls=%fused_computation.23 | convolution fusion | flops 103809024 | bytes 2299904 | tf_op jit(solution)/shard_map/dot_general | solution.py:35
  165.9 2.0 fusion.39
  167.9 2.2 all-to-all-done.3
  172.8 10.6 %all-to-all-start.4 = ((f32[64,1,384]{2,1,0:T(1,128)}), f32[64,1,384]{2,1,0:T(1,128)S(1)}, u32[]{:S(2)}, u32[]{:S(2)}) async-start(f32[64,1,384]{2,1,0:T(1,128)} %broadcast_in_dim.110), calls=%async_computation.4 | async-start | bytes 196608 | tf_op jit(solution)/shard_map/all_to_all | solution.py:51
  183.5 2.5 %scatter_fusion.1 = f32[1024,16]{1,0:T(8,128)} fusion(f32[1024,16]{1,0:T(8,128)} %get-tuple-element.42, s32[24]{0:T(128)S(1)} %copy-done.30, f32[24,16]{1,0:T(8,128)S(1)} %copy.123), kind=kCustom, calls=%fused_computation.11 | custom fusion | flops 384 | bytes 4704 | tf_op jit(solution)/shard_map/scatter-add | solution.py:168
  188.7 7.0 %all-to-all-done.4 = f32[64,1,384]{2,1,0:T(1,128)S(1)} async-done(((f32[64,1,384]{2,1,0:T(1,128)}), f32[64,1,384]{2,1,0:T(1,128)S(1)}, u32[]{:S(2)}, u32[]{:S(2)}) %all-to-all-start.4) | async-done | bytes 98336 | tf_op jit(solution)/shard_map/all_to_all | solution.py:51
  204.9 7.7 %collective-permute-done.6 = f32[512,16]{0,1:T(8,128)S(1)} collective-permute-done((f32[512,16]{0,1:T(8,128)S(1)}, f32[512,16]{0,1:T(8,128)S(1)}, u32[]{:S(2)}, u32[]{:S(2)}) %collective-permute-start.6) | collective-permute-done | bytes 32800 | tf_op jit(solution)/shard_map/ppermute | solution.py:17
  213.2 7.7 %psum.7 = f32[512]{0:T(512)S(1)} all-reduce(f32[512]{0:T(512)S(1)} %get-tuple-element.34), channel_id=1, replica_groups=mesh['blk'=64,'path'=4] {'path'}, use_global_device_ids=true, to_apply=%region_14.15 | all-reduce | flops 512 | bytes 4096 | tf_op jit(solution)/shard_map/psum | solution.py:191
  (220 shorter events, 79.3 us)
Async XLA Ops:
  0.6 36.2 %copy-start = (bf16[512,1024]{1,0:T(8,128)(2,1)S(1)}, bf16[512,1024]{1,0:T(8,128)(2,1)}, u32[]{:S(2)}) copy-start(bf16[512,1024]{1,0:T(8,128)(2,1)} %param.17) | copy-start | bytes 3145732
  2.4 62.1 %copy-start.14 = (f32[1024,32]{0,1:T(8,128)}, f32[1024,32]{0,1:T(8,128)S(1)}, u32[]{:S(2)}) copy-start(f32[1024,32]{0,1:T(8,128)S(1)} %get-tuple-element.46) | copy-start | bytes 393220
  2.4 62.1 %collective-permute-start = (f32[1024,32]{0,1:T(8,128)S(1)}, f32[1024,32]{0,1:T(8,128)}, u32[]{:S(2)}, u32[]{:S(2)}) collective-permute-start(f32[1024,32]{0,1:T(8,128)S(1)} %get-tuple-element.46), channel_id=1, source_target_pairs={{0,1},{1,2},{2,3},{3,0},{4,5},{5,6},{6,7},{7,4},{8,9},{9,10},{10,1... | collective-permute-start | bytes 393224 | tf_op jit(solution)/shard_map/ppermute | solution.py:17
  5.0 59.6 %collective-permute-start.1 = (f32[1024,32]{0,1:T(8,128)S(1)}, f32[1024,32]{0,1:T(8,128)}, u32[]{:S(2)}, u32[]{:S(2)}) collective-permute-start(f32[1024,32]{0,1:T(8,128)S(1)} %get-tuple-element.46), channel_id=1, source_target_pairs={{0,2},{1,3},{2,0},{3,1},{4,6},{5,7},{6,4},{7,5},{8,10},{9,11},{10,... | collective-permute-start | bytes 393224 | tf_op jit(solution)/shard_map/ppermute | solution.py:17
  8.0 56.6 %collective-permute-start.2 = (f32[1024,32]{0,1:T(8,128)S(1)}, f32[1024,32]{0,1:T(8,128)}, u32[]{:S(2)}, u32[]{:S(2)}) collective-permute-start(f32[1024,32]{0,1:T(8,128)S(1)} %get-tuple-element.46), channel_id=1, source_target_pairs={{0,3},{1,0},{2,1},{3,2},{4,7},{5,4},{6,5},{7,6},{8,11},{9,8},{10,9... | collective-permute-start | bytes 393224 | tf_op jit(solution)/shard_map/ppermute | solution.py:17
  10.4 42.7 %copy-start.27 = (s32[1024]{0:T(1024)}, s32[1024]{0:T(1024)S(1)}, u32[]{:S(2)}) copy-start(s32[1024]{0:T(1024)S(1)} %get-tuple-element.64) | copy-start | bytes 12292
  13.7 55.5 %all-to-all-start = ((bf16[64,18,512]{2,1,0:T(8,128)(2,1)}), bf16[64,18,512]{2,1,0:T(8,128)(2,1)S(1)}, u32[]{:S(2)}, u32[]{:S(2)}) async-start(bf16[64,18,512]{2,1,0:T(8,128)(2,1)} %broadcast_in_dim.57), calls=%async_computation | async-start | bytes 3145728 | tf_op jit(solution)/shard_map/all_to_all | solution.py:58
  31.0 32.8 %copy-start.11 = (bf16[72,512]{1,0:T(8,128)(2,1)}, bf16[72,512]{1,0:T(8,128)(2,1)S(1)}, u32[]{:S(2)}) copy-start(bf16[72,512]{1,0:T(8,128)(2,1)S(1)} %gather_fusion.4) | copy-start | bytes 221188
  77.1 41.2 %all-to-all-start.1 = ((f32[64,1,2304]{2,1,0:T(1,128)}), f32[64,1,2304]{2,1,0:T(1,128)}, u32[]{:S(2)}, u32[]{:S(2)}) async-start(f32[64,1,2304]{2,1,0:T(1,128)} %bitcast.143), calls=%async_computation.1 | async-start | bytes 1179648 | tf_op jit(solution)/shard_map/all_to_all | solution.py:72
  90.1 40.8 %collective-permute-start.7 = (bf16[512,512]{1,0:T(8,128)(2,1)S(1)}, bf16[512,512]{1,0:T(8,128)(2,1)}, u32[]{:S(2)}, u32[]{:S(2)}) collective-permute-start(bf16[512,512]{1,0:T(8,128)(2,1)S(1)} %copy-done.4), channel_id=1, source_target_pairs={{0,4},{4,8},{8,12},{12,16},{16,20},{20,24},{24,28},{28,32},{32,36}... | collective-permute-start | bytes 1572872 | tf_op jit(solution)/shard_map/ppermute | solution.py:17
  98.4 26.7 %copy-start.40 = (pred[4]{0:T(512)(128)(4,1)S(1)}, pred[4]{0:T(512)(128)(4,1)}, u32[]{:S(2)}) copy-start(pred[4]{0:T(512)(128)(4,1)} %compare_and_fusion) | copy-start | bytes 16
  101.5 9.6 %collective-permute-start.3 = (f32[3,24,384]{2,1,0:T(8,128)S(1)}, f32[3,24,384]{2,1,0:T(8,128)S(1)}, u32[]{:S(2)}, u32[]{:S(2)}) collective-permute-start(f32[3,24,384]{2,1,0:T(8,128)S(1)} %get-tuple-element.45), channel_id=1, source_target_pairs={{0,1},{1,2},{2,3},{3,0},{4,5},{5,6},{6,7},{7,4},{8,9},{9,10},{10,1... | collective-permute-start | bytes 331784 | tf_op jit(solution)/shard_map/ppermute | solution.py:17
  101.6 14.2 %collective-permute-start.4 = (f32[3,24,384]{2,1,0:T(8,128)S(1)}, f32[3,24,384]{2,1,0:T(8,128)S(1)}, u32[]{:S(2)}, u32[]{:S(2)}) collective-permute-start(f32[3,24,384]{2,1,0:T(8,128)S(1)} %get-tuple-element.45), channel_id=1, source_target_pairs={{0,2},{1,3},{2,0},{3,1},{4,6},{5,7},{6,4},{7,5},{8,10},{9,11},{10,... | collective-permute-start | bytes 331784 | tf_op jit(solution)/shard_map/ppermute | solution.py:17
  102.8 12.9 %collective-permute-start.5 = (f32[3,24,384]{2,1,0:T(8,128)S(1)}, f32[3,24,384]{2,1,0:T(8,128)S(1)}, u32[]{:S(2)}, u32[]{:S(2)}) collective-permute-start(f32[3,24,384]{2,1,0:T(8,128)S(1)} %get-tuple-element.45), channel_id=1, source_target_pairs={{0,3},{1,0},{2,1},{3,2},{4,7},{5,4},{6,5},{7,6},{8,11},{9,8},{10,9... | collective-permute-start | bytes 331784 | tf_op jit(solution)/shard_map/ppermute | solution.py:17
  120.5 9.0 %all-to-all-start.2 = ((f32[4,1,576]{2,1,0:T(1,128)}), f32[4,1,576]{2,1,0:T(1,128)S(1)}, u32[]{:S(2)}, u32[]{:S(2)}) async-start(f32[4,1,576]{2,1,0:T(1,128)} %reshape.442), calls=%async_computation.2 | async-start | bytes 20480 | tf_op jit(solution)/shard_map/all_to_all | solution.py:124
  132.2 25.9 %copy-start.7 = (f32[1024,16]{1,0:T(8,128)S(1)}, f32[1024,16]{1,0:T(8,128)}, u32[]{:S(2)}) copy-start(f32[1024,16]{1,0:T(8,128)} %copy.109) | copy-start | bytes 196612
  132.2 25.9 %copy-start.32 = (s32[24]{0:T(128)S(1)}, s32[24]{0:T(128)}, u32[]{:S(2)}) copy-start(s32[24]{0:T(128)} %copy-done.31) | copy-start | bytes 292
  132.2 26.8 %copy-start.6 = (f32[1024,16]{1,0:T(8,128)S(1)}, f32[1024,16]{1,0:T(8,128)}, u32[]{:S(2)}) copy-start(f32[1024,16]{1,0:T(8,128)} %copy-done.5) | copy-start | bytes 196612
  135.4 26.8 %copy-start.15 = (f32[1024,32]{0,1:T(8,128)S(1)}, f32[1024,32]{0,1:T(8,128)}, u32[]{:S(2)}) copy-start(f32[1024,32]{0,1:T(8,128)} %copy-done.14) | copy-start | bytes 393220
  135.4 26.8 %copy-start.36 = (f32[1024]{0:T(1024)S(1)}, f32[1024]{0:T(1024)}, u32[]{:S(2)}) copy-start(f32[1024]{0:T(1024)} %copy-done.34) | copy-start | bytes 12292
  136.6 33.5 %all-to-all-start.3 = ((f32[64,1,384]{2,1,0:T(1,128)}), f32[64,1,384]{2,1,0:T(1,128)S(1)}, u32[]{:S(2)}, u32[]{:S(2)}) async-start(f32[64,1,384]{2,1,0:T(1,128)} %broadcast_in_dim.107), calls=%async_computation.3 | async-start | bytes 196608 | tf_op jit(solution)/shard_map/all_to_all | solution.py:51
  172.8 22.8 %all-to-all-start.4 = ((f32[64,1,384]{2,1,0:T(1,128)}), f32[64,1,384]{2,1,0:T(1,128)S(1)}, u32[]{:S(2)}, u32[]{:S(2)}) async-start(f32[64,1,384]{2,1,0:T(1,128)} %broadcast_in_dim.110), calls=%async_computation.4 | async-start | bytes 196608 | tf_op jit(solution)/shard_map/all_to_all | solution.py:51
  199.9 4.9 %collective-permute-start.8 = (f32[512,16]{0,1:T(8,128)S(1)}, f32[512,16]{0,1:T(8,128)S(1)}, u32[]{:S(2)}, u32[]{:S(2)}) collective-permute-start(f32[512,16]{0,1:T(8,128)S(1)} %fusion.58), channel_id=1, source_target_pairs={{0,4},{4,8},{8,12},{12,16},{16,20},{20,24},{24,28},{28,32},{32,36}... | collective-permute-start | bytes 98312 | tf_op jit(solution)/shard_map/ppermute | solution.py:17
  201.6 11.0 %collective-permute-start.6 = (f32[512,16]{0,1:T(8,128)S(1)}, f32[512,16]{0,1:T(8,128)S(1)}, u32[]{:S(2)}, u32[]{:S(2)}) collective-permute-start(f32[512,16]{0,1:T(8,128)S(1)} %fusion.60), channel_id=1, source_target_pairs={{0,8},{4,12},{8,16},{12,20},{16,24},{20,28},{24,32},{28,36},{32,40... | collective-permute-start | bytes 98312 | tf_op jit(solution)/shard_map/ppermute | solution.py:17
  (35 other events, 333.5 us)

commit v5 on v4

--- a/solution.py
+++ b/solution.py
@@ -188,7 +188,7 @@
     next_term = next_sum / root_count
     scores = passed_along(first_part, "blk", 2) + passed_along(next_term, "blk", 1)
     squares_local = jnp.sum(scores * scores, axis=1)
-    summed = lax.psum(squares_local, "path")
+    summed = jnp.sum(gather_blocks(squares_local, "path"), axis=0)
     path_rms = jnp.sqrt(summed / (scores.shape[1] * lax.axis_size("path")) + EPSILON)
     return (coefficients, velocity, scores, path_rms)
 

time: 224 us -> 224 us (level)
  waiting for transfers between devices: 29.9 us -> 37.7 us
  blocking collectives: 7.75 us -> 0 us
  starting transfers between devices: 76.5 us -> 79.7 us
    psum x1 -> x0, blocking collectives: 7.75 us -> none  [shards(): summed = lax.psum(squares_local, 'path')]
    all_to_all x2 -> x3, waiting for transfers between devices: 9.15 us -> 14.2 us  [gather_blocks(): got = lax.all_to_all(spread, axis, 0, 0, tiled=True)]
    all_to_all x2 -> x3, starting transfers between devices: 32 us -> 35.3 us  [gather_blocks(): got = lax.all_to_all(spread, axis, 0, 0, tiled=True)]
    ppermute x9, waiting for transfers between devices: 17.2 us -> 20 us  [passed_along(): lax.ppermute(shard, axis, [(i, (i + by) % length) for i in range(length)])]
    unnamed x102 -> x106, local copies, waits for them, and re-layouts: 6.25 us -> 6.26 us
  transfers between devices with their start and end apart: 14 -> 15, of which waited for: 6 -> 7; matrix products, arithmetic and copies ran while one was open for 37% -> 35% of each run, Pallas kernels for 0% -> 0%
where the time goes in v5:
time: 224 us; the launch traced here: 222 us
  starting transfers between devices  79.7 us (36%)
  local copies, waits for them, and re-layouts  40 us (18%)
  matrix products  38.8 us (17%)
  waiting for transfers between devices  37.7 us (17%)
  other arithmetic  24.7 us (11%)
    all_to_all x3, starting transfers between devices, gather_blocks(): got = lax.all_to_all(spread, axis, 0, 0, tiled=True)  35.3 us
    ppermute x9, waiting for transfers between devices, passed_along(): lax.ppermute(shard, axis, [(i, (i + by) % length) for i in range(length)])  20 us
    all_to_all x3, waiting for transfers between devices, gather_blocks(): got = lax.all_to_all(spread, axis, 0, 0, tiled=True)  14.2 us
    all_to_all x1, starting transfers between devices, gather_stack(): return lax.all_to_all(spread, axis, 0, 0, tiled=True)  14 us
    dot_general x8, matrix products, kernel_tile_of(): lax.dot_general(left_rows, right_rows, (((1,), (1,)), ((), ())), preferre...  13 us
    all_to_all x1, starting transfers between devices, sum_to_owners(): got = lax.all_to_all(flat, axis, 0, 0, tiled=True)  13 us
    ppermute x9, starting transfers between devices, passed_along(): lax.ppermute(shard, axis, [(i, (i + by) % length) for i in range(length)])  12.9 us
    dot_general x1, matrix products, prior_values(): return jnp.dot(features, prior_weight, precision=lax.Precision.HIGHEST)  10.1 us
  transfers between devices with their start and end apart: 15, of which 7 were waited for; matrix products, arithmetic and copies ran while one was open for 35% of the time, Pallas kernels for 0%

profile of v5, /device:TPU:1, one launch (start us, length us, event | category | flops | bytes accessed | tf_op | source)
XLA Modules:
  0.0 222.3 jit_solution(6646050182901295727)
XLA Ops:
  2.4 2.5 %collective-permute-start = (f32[1024,32]{0,1:T(8,128)S(1)}, f32[1024,32]{0,1:T(8,128)}, u32[]{:S(2)}, u32[]{:S(2)}) collective-permute-start(f32[1024,32]{0,1:T(8,128)S(1)} %get-tuple-element.54), channel_id=1, source_target_pairs={{0,1},{1,2},{2,3},{3,0},{4,5},{5,6},{6,7},{7,4},{8,9},{9,10},{10,1... | collective-permute-start | bytes 393224 | tf_op jit(solution)/shard_map/ppermute | solution.py:17
  5.0 3.0 %collective-permute-start.1 = (f32[1024,32]{0,1:T(8,128)S(1)}, f32[1024,32]{0,1:T(8,128)}, u32[]{:S(2)}, u32[]{:S(2)}) collective-permute-start(f32[1024,32]{0,1:T(8,128)S(1)} %get-tuple-element.54), channel_id=1, source_target_pairs={{0,2},{1,3},{2,0},{3,1},{4,6},{5,7},{6,4},{7,5},{8,10},{9,11},{10,... | collective-permute-start | bytes 393224 | tf_op jit(solution)/shard_map/ppermute | solution.py:17
  11.0 2.0 gather_fusion
  14.2 14.0 %all-to-all-start = ((bf16[64,18,512]{2,1,0:T(8,128)(2,1)}), bf16[64,18,512]{2,1,0:T(8,128)(2,1)S(1)}, u32[]{:S(2)}, u32[]{:S(2)}) async-start(bf16[64,18,512]{2,1,0:T(8,128)(2,1)} %broadcast_in_dim.59), calls=%async_computation | async-start | bytes 3145728 | tf_op jit(solution)/shard_map/all_to_all | solution.py:58
  29.5 2.1 gather_fusion.4
  38.2 10.1 %fusion.24 = f32[512,16]{0,1:T(8,128)} fusion(f32[1024,16]{0,1:T(8,128)S(1)} %copy-done.19, f32[512,1024]{1,0:T(8,128)S(1)} %fusion.118, f32[1024]{0:T(1024)S(1)} %copy-done.34), kind=kOutput, calls=%fused_computation.40 | convolution fusion | flops 102236160 | bytes 2199552 | tf_op jit(solution)/shard_map/dot_general | solution.py:44
  49.1 2.1 fusion.16
  70.9 3.1 %fusion = f32[1152,1024]{1,0:T(8,128)S(1)} fusion(bf16[1152,512]{1,0:T(8,128)(2,1)} %reshape.333, bf16[1024,512]{1,0:T(8,128)(2,1)} %param.10, f32[1024]{0:T(1024)S(1)} %copy-done.36, f32[1152]{0:T(1024)S(1)} %add.295), kind=kOutput, calls=%fused_computation.14 | convolution fusion | flops 1211498496 | bytes 6955520 | tf_op jit(solution)/shard_map/dot_general | solution.py:26
  74.0 3.2 %fusion.1 = f32[1152,128]{1,0:T(8,128)} fusion(f32[1024,128]{0,1:T(8,128)S(1)} %bitcast.144, f32[1152,1024]{1,0:T(8,128)S(1)} %fusion), kind=kOutput, calls=%fused_computation.15 | convolution fusion | flops 909508608 | bytes 5832704 | tf_op jit(solution)/shard_map/dot_general | solution.py:35
  77.1 13.0 %all-to-all-start.1 = ((f32[64,1,2304]{2,1,0:T(1,128)}), f32[64,1,2304]{2,1,0:T(1,128)}, u32[]{:S(2)}, u32[]{:S(2)}) async-start(f32[64,1,2304]{2,1,0:T(1,128)} %bitcast.143), calls=%async_computation.1 | async-start | bytes 1179648 | tf_op jit(solution)/shard_map/all_to_all | solution.py:72
  102.8 2.3 %collective-permute-start.5 = (f32[3,24,384]{2,1,0:T(8,128)S(1)}, f32[3,24,384]{2,1,0:T(8,128)S(1)}, u32[]{:S(2)}, u32[]{:S(2)}) collective-permute-start(f32[3,24,384]{2,1,0:T(8,128)S(1)} %get-tuple-element.53), channel_id=1, source_target_pairs={{0,3},{1,0},{2,1},{3,2},{4,7},{5,4},{6,5},{7,6},{8,11},{9,8},{10,9... | collective-permute-start | bytes 331784 | tf_op jit(solution)/shard_map/ppermute | solution.py:17
  106.4 4.7 %collective-permute-done.3 = f32[3,24,384]{2,1,0:T(8,128)S(1)} collective-permute-done((f32[3,24,384]{2,1,0:T(8,128)S(1)}, f32[3,24,384]{2,1,0:T(8,128)S(1)}, u32[]{:S(2)}, u32[]{:S(2)}) %collective-permute-start.3) | collective-permute-done | bytes 110624 | tf_op jit(solution)/shard_map/ppermute | solution.py:17
  111.1 4.7 %collective-permute-done.4 = f32[3,24,384]{2,1,0:T(8,128)S(1)} collective-permute-done((f32[3,24,384]{2,1,0:T(8,128)S(1)}, f32[3,24,384]{2,1,0:T(8,128)S(1)}, u32[]{:S(2)}, u32[]{:S(2)}) %collective-permute-start.4) | collective-permute-done | bytes 110624 | tf_op jit(solution)/shard_map/ppermute | solution.py:17
  120.5 4.6 %all-to-all-start.2 = ((f32[4,1,576]{2,1,0:T(1,128)}), f32[4,1,576]{2,1,0:T(1,128)S(1)}, u32[]{:S(2)}, u32[]{:S(2)}) async-start(f32[4,1,576]{2,1,0:T(1,128)} %reshape.449), calls=%async_computation.2 | async-start | bytes 20480 | tf_op jit(solution)/shard_map/all_to_all | solution.py:124
  126.0 3.6 %all-to-all-done.2 = f32[4,1,576]{2,1,0:T(1,128)S(1)} async-done(((f32[4,1,576]{2,1,0:T(1,128)}), f32[4,1,576]{2,1,0:T(1,128)S(1)}, u32[]{:S(2)}, u32[]{:S(2)}) %all-to-all-start.2) | async-done | bytes 9248 | tf_op jit(solution)/shard_map/all_to_all | solution.py:124
  132.2 3.2 %fusion.120 = f32[512,1024]{1,0:T(8,128)} fusion(bf16[512,512]{1,0:T(8,128)(2,1)} %collective-permute-done.7, bf16[1024,512]{1,0:T(8,128)(2,1)S(1)} %copy-done.2), kind=kOutput, calls=%fused_computation.205 | convolution fusion | flops 536870912 | bytes 3670016 | tf_op jit(solution)/shard_map/dot_general | solution.py:26
  136.6 21.3 %all-to-all-start.3 = ((f32[64,1,384]{2,1,0:T(1,128)}), f32[64,1,384]{2,1,0:T(1,128)S(1)}, u32[]{:S(2)}, u32[]{:S(2)}) async-start(f32[64,1,384]{2,1,0:T(1,128)} %broadcast_in_dim.112), calls=%async_computation.3 | async-start | bytes 196608 | tf_op jit(solution)/shard_map/all_to_all | solution.py:51
  162.3 3.7 %fusion.8 = f32[512,32]{0,1:T(8,128)} fusion(f32[1024,32]{0,1:T(8,128)S(1)} %copy-done.16, f32[512,1024]{1,0:T(8,128)} %fusion.120, f32[512]{0:T(512)S(1)} %multiply_reduce_fusion.2, f32[1024]{0:T(1024)S(1)} %copy-done.37), kind=kOutput, calls=%fused_computation.23 | convolution fusion | flops 103809024 | bytes 2299904 | tf_op jit(solution)/shard_map/dot_general | solution.py:35
  165.9 2.1 fusion.39
  168.0 2.1 all-to-all-done.3
  172.9 10.7 %all-to-all-start.4 = ((f32[64,1,384]{2,1,0:T(1,128)}), f32[64,1,384]{2,1,0:T(1,128)S(1)}, u32[]{:S(2)}, u32[]{:S(2)}) async-start(f32[64,1,384]{2,1,0:T(1,128)} %broadcast_in_dim.115), calls=%async_computation.4 | async-start | bytes 196608 | tf_op jit(solution)/shard_map/all_to_all | solution.py:51
  185.4 10.3 %all-to-all-done.4 = f32[64,1,384]{2,1,0:T(1,128)S(1)} async-done(((f32[64,1,384]{2,1,0:T(1,128)}), f32[64,1,384]{2,1,0:T(1,128)S(1)}, u32[]{:S(2)}, u32[]{:S(2)}) %all-to-all-start.4) | async-done | bytes 98336 | tf_op jit(solution)/shard_map/all_to_all | solution.py:51
  202.3 10.5 %collective-permute-done.6 = f32[512,16]{0,1:T(8,128)S(1)} collective-permute-done((f32[512,16]{0,1:T(8,128)S(1)}, f32[512,16]{0,1:T(8,128)S(1)}, u32[]{:S(2)}, u32[]{:S(2)}) %collective-permute-start.6) | collective-permute-done | bytes 32800 | tf_op jit(solution)/shard_map/ppermute | solution.py:17
  214.0 3.2 %all-to-all-start.5 = ((f32[4,1,512]{2,1,0:T(1,128)}), f32[4,1,512]{2,1,0:T(1,128)S(1)}, u32[]{:S(2)}, u32[]{:S(2)}) async-start(f32[4,1,512]{2,1,0:T(1,128)} %broadcast_in_dim.116), calls=%async_computation.5 | async-start | bytes 16384 | tf_op jit(solution)/shard_map/all_to_all | solution.py:51
  (227 shorter events, 79.0 us)
Async XLA Ops:
  0.6 36.9 %copy-start = (bf16[512,1024]{1,0:T(8,128)(2,1)S(1)}, bf16[512,1024]{1,0:T(8,128)(2,1)}, u32[]{:S(2)}) copy-start(bf16[512,1024]{1,0:T(8,128)(2,1)} %param.17) | copy-start | bytes 3145732
  2.4 62.1 %copy-start.15 = (f32[1024,32]{0,1:T(8,128)}, f32[1024,32]{0,1:T(8,128)S(1)}, u32[]{:S(2)}) copy-start(f32[1024,32]{0,1:T(8,128)S(1)} %get-tuple-element.54) | copy-start | bytes 393220
  2.4 62.1 %collective-permute-start = (f32[1024,32]{0,1:T(8,128)S(1)}, f32[1024,32]{0,1:T(8,128)}, u32[]{:S(2)}, u32[]{:S(2)}) collective-permute-start(f32[1024,32]{0,1:T(8,128)S(1)} %get-tuple-element.54), channel_id=1, source_target_pairs={{0,1},{1,2},{2,3},{3,0},{4,5},{5,6},{6,7},{7,4},{8,9},{9,10},{10,1... | collective-permute-start | bytes 393224 | tf_op jit(solution)/shard_map/ppermute | solution.py:17
  5.0 59.6 %collective-permute-start.1 = (f32[1024,32]{0,1:T(8,128)S(1)}, f32[1024,32]{0,1:T(8,128)}, u32[]{:S(2)}, u32[]{:S(2)}) collective-permute-start(f32[1024,32]{0,1:T(8,128)S(1)} %get-tuple-element.54), channel_id=1, source_target_pairs={{0,2},{1,3},{2,0},{3,1},{4,6},{5,7},{6,4},{7,5},{8,10},{9,11},{10,... | collective-permute-start | bytes 393224 | tf_op jit(solution)/shard_map/ppermute | solution.py:17
  8.0 56.6 %collective-permute-start.2 = (f32[1024,32]{0,1:T(8,128)S(1)}, f32[1024,32]{0,1:T(8,128)}, u32[]{:S(2)}, u32[]{:S(2)}) collective-permute-start(f32[1024,32]{0,1:T(8,128)S(1)} %get-tuple-element.54), channel_id=1, source_target_pairs={{0,3},{1,0},{2,1},{3,2},{4,7},{5,4},{6,5},{7,6},{8,11},{9,8},{10,9... | collective-permute-start | bytes 393224 | tf_op jit(solution)/shard_map/ppermute | solution.py:17
  14.2 54.9 %all-to-all-start = ((bf16[64,18,512]{2,1,0:T(8,128)(2,1)}), bf16[64,18,512]{2,1,0:T(8,128)(2,1)S(1)}, u32[]{:S(2)}, u32[]{:S(2)}) async-start(bf16[64,18,512]{2,1,0:T(8,128)(2,1)} %broadcast_in_dim.59), calls=%async_computation | async-start | bytes 3145728 | tf_op jit(solution)/shard_map/all_to_all | solution.py:58
  31.6 32.2 %copy-start.12 = (bf16[72,512]{1,0:T(8,128)(2,1)}, bf16[72,512]{1,0:T(8,128)(2,1)S(1)}, u32[]{:S(2)}) copy-start(bf16[72,512]{1,0:T(8,128)(2,1)S(1)} %gather_fusion.4) | copy-start | bytes 221188
  33.1 27.2 %copy-start.27 = (s32[1024]{0:T(1024)}, s32[1024]{0:T(1024)S(1)}, u32[]{:S(2)}) copy-start(s32[1024]{0:T(1024)S(1)} %get-tuple-element.71) | copy-start | bytes 12292
  77.1 41.2 %all-to-all-start.1 = ((f32[64,1,2304]{2,1,0:T(1,128)}), f32[64,1,2304]{2,1,0:T(1,128)}, u32[]{:S(2)}, u32[]{:S(2)}) async-start(f32[64,1,2304]{2,1,0:T(1,128)} %bitcast.143), calls=%async_computation.1 | async-start | bytes 1179648 | tf_op jit(solution)/shard_map/all_to_all | solution.py:72
  90.1 40.8 %collective-permute-start.7 = (bf16[512,512]{1,0:T(8,128)(2,1)S(1)}, bf16[512,512]{1,0:T(8,128)(2,1)}, u32[]{:S(2)}, u32[]{:S(2)}) collective-permute-start(bf16[512,512]{1,0:T(8,128)(2,1)S(1)} %copy-done.4), channel_id=1, source_target_pairs={{0,4},{4,8},{8,12},{12,16},{16,20},{20,24},{24,28},{28,32},{32,36}... | collective-permute-start | bytes 1572872 | tf_op jit(solution)/shard_map/ppermute | solution.py:17
  98.4 26.7 %copy-start.41 = (pred[4]{0:T(512)(128)(4,1)S(1)}, pred[4]{0:T(512)(128)(4,1)}, u32[]{:S(2)}) copy-start(pred[4]{0:T(512)(128)(4,1)} %compare_and_fusion) | copy-start | bytes 16
  101.5 9.6 %collective-permute-start.3 = (f32[3,24,384]{2,1,0:T(8,128)S(1)}, f32[3,24,384]{2,1,0:T(8,128)S(1)}, u32[]{:S(2)}, u32[]{:S(2)}) collective-permute-start(f32[3,24,384]{2,1,0:T(8,128)S(1)} %get-tuple-element.53), channel_id=1, source_target_pairs={{0,1},{1,2},{2,3},{3,0},{4,5},{5,6},{6,7},{7,4},{8,9},{9,10},{10,1... | collective-permute-start | bytes 331784 | tf_op jit(solution)/shard_map/ppermute | solution.py:17
  101.6 14.2 %collective-permute-start.4 = (f32[3,24,384]{2,1,0:T(8,128)S(1)}, f32[3,24,384]{2,1,0:T(8,128)S(1)}, u32[]{:S(2)}, u32[]{:S(2)}) collective-permute-start(f32[3,24,384]{2,1,0:T(8,128)S(1)} %get-tuple-element.53), channel_id=1, source_target_pairs={{0,2},{1,3},{2,0},{3,1},{4,6},{5,7},{6,4},{7,5},{8,10},{9,11},{10,... | collective-permute-start | bytes 331784 | tf_op jit(solution)/shard_map/ppermute | solution.py:17
  102.8 13.0 %collective-permute-start.5 = (f32[3,24,384]{2,1,0:T(8,128)S(1)}, f32[3,24,384]{2,1,0:T(8,128)S(1)}, u32[]{:S(2)}, u32[]{:S(2)}) collective-permute-start(f32[3,24,384]{2,1,0:T(8,128)S(1)} %get-tuple-element.53), channel_id=1, source_target_pairs={{0,3},{1,0},{2,1},{3,2},{4,7},{5,4},{6,5},{7,6},{8,11},{9,8},{10,9... | collective-permute-start | bytes 331784 | tf_op jit(solution)/shard_map/ppermute | solution.py:17
  120.5 9.0 %all-to-all-start.2 = ((f32[4,1,576]{2,1,0:T(1,128)}), f32[4,1,576]{2,1,0:T(1,128)S(1)}, u32[]{:S(2)}, u32[]{:S(2)}) async-start(f32[4,1,576]{2,1,0:T(1,128)} %reshape.449), calls=%async_computation.2 | async-start | bytes 20480 | tf_op jit(solution)/shard_map/all_to_all | solution.py:124
  132.2 26.8 %copy-start.6 = (f32[1024,16]{1,0:T(8,128)S(1)}, f32[1024,16]{1,0:T(8,128)}, u32[]{:S(2)}) copy-start(f32[1024,16]{1,0:T(8,128)} %copy-done.5) | copy-start | bytes 196612
  135.4 26.8 %copy-start.16 = (f32[1024,32]{0,1:T(8,128)S(1)}, f32[1024,32]{0,1:T(8,128)}, u32[]{:S(2)}) copy-start(f32[1024,32]{0,1:T(8,128)} %copy-done.15) | copy-start | bytes 393220
  135.4 26.8 %copy-start.37 = (f32[1024]{0:T(1024)S(1)}, f32[1024]{0:T(1024)}, u32[]{:S(2)}) copy-start(f32[1024]{0:T(1024)} %copy-done.35) | copy-start | bytes 12292
  136.6 33.5 %all-to-all-start.3 = ((f32[64,1,384]{2,1,0:T(1,128)}), f32[64,1,384]{2,1,0:T(1,128)S(1)}, u32[]{:S(2)}, u32[]{:S(2)}) async-start(f32[64,1,384]{2,1,0:T(1,128)} %broadcast_in_dim.112), calls=%async_computation.3 | async-start | bytes 196608 | tf_op jit(solution)/shard_map/all_to_all | solution.py:51
  172.9 22.8 %all-to-all-start.4 = ((f32[64,1,384]{2,1,0:T(1,128)}), f32[64,1,384]{2,1,0:T(1,128)S(1)}, u32[]{:S(2)}, u32[]{:S(2)}) async-start(f32[64,1,384]{2,1,0:T(1,128)} %broadcast_in_dim.115), calls=%async_computation.4 | async-start | bytes 196608 | tf_op jit(solution)/shard_map/all_to_all | solution.py:51
  184.6 32.7 %copy-start.29 = (s32[24]{0:T(128)S(1)}, s32[24]{0:T(128)}, u32[]{:S(2)}) copy-start(s32[24]{0:T(128)} %copy-done.28) | copy-start | bytes 292
  200.2 2.1 collective-permute-start.8
  201.8 11.0 %collective-permute-start.6 = (f32[512,16]{0,1:T(8,128)S(1)}, f32[512,16]{0,1:T(8,128)S(1)}, u32[]{:S(2)}, u32[]{:S(2)}) collective-permute-start(f32[512,16]{0,1:T(8,128)S(1)} %fusion.60), channel_id=1, source_target_pairs={{0,8},{4,12},{8,16},{12,20},{16,24},{20,28},{24,32},{28,36},{32,40... | collective-permute-start | bytes 98312 | tf_op jit(solution)/shard_map/ppermute | solution.py:17
  214.0 7.7 %all-to-all-start.5 = ((f32[4,1,512]{2,1,0:T(1,128)}), f32[4,1,512]{2,1,0:T(1,128)S(1)}, u32[]{:S(2)}, u32[]{:S(2)}) async-start(f32[4,1,512]{2,1,0:T(1,128)} %broadcast_in_dim.116), calls=%async_computation.5 | async-start | bytes 16384 | tf_op jit(solution)/shard_map/all_to_all | solution.py:51
  (38 other events, 413.3 us)

commit v6 on v5

--- a/solution.py
+++ b/solution.py
@@ -131,7 +131,8 @@
         mine = own_rows[t * slot_count:(t + 1) * slot_count]
         theirs = gathered[:, s * share:(s + 1) * share].reshape(n_blk * share, -1)
         tiles.append(kernel_tile_of(mine, square_norms(mine), theirs, square_norms(theirs)))
-    tiles = gather_by_permutes(jnp.stack(tiles), "path")
+    tiles, _ = lax.optimization_barrier((jnp.stack(tiles), start_sums))
+    tiles = gather_by_permutes(tiles, "path")
     tile_of = {pair: tiles[:, k] for k, pair in enumerate(pairs)}
 
     neighbour, _ = lax.optimization_barrier((neighbour, start_sums))

time: 224 us -> 205 us (0.915)
  starting transfers between devices: 79.7 us -> 69.8 us
  other arithmetic: 24.7 us -> 22.1 us
  matrix products: 38.8 us -> 36.2 us
  local copies, waits for them, and re-layouts: 40 us -> 37.7 us
    all_to_all x3, starting transfers between devices: 35.3 us -> 23.4 us  [gather_blocks(): got = lax.all_to_all(spread, axis, 0, 0, tiled=True)]
    ppermute x9, waiting for transfers between devices: 20 us -> 11.4 us  [passed_along(): lax.ppermute(shard, axis, [(i, (i + by) % length) for i in range(length)])]
    all_to_all x1, waiting for transfers between devices: 0.01 us -> 4.93 us  [gather_stack(): return lax.all_to_all(spread, axis, 0, 0, tiled=True)]
    all_to_all x1, starting transfers between devices: 13 us -> 16.5 us  [sum_to_owners(): got = lax.all_to_all(flat, axis, 0, 0, tiled=True)]
    unnamed x106 -> x90, local copies, waits for them, and re-layouts: 6.26 us -> 7.72 us
  transfers between devices with their start and end apart: 15 -> 15, of which waited for: 7 -> 6; matrix products, arithmetic and copies ran while one was open for 35% -> 37% of each run, Pallas kernels for 0% -> 0%
where the time goes in v6:
time: 205 us; the launch traced here: 203 us
  starting transfers between devices  69.8 us (34%)
  local copies, waits for them, and re-layouts  37.7 us (18%)
  matrix products  36.2 us (18%)
  waiting for transfers between devices  36.1 us (18%)
  other arithmetic  22.1 us (11%)
    all_to_all x3, starting transfers between devices, gather_blocks(): got = lax.all_to_all(spread, axis, 0, 0, tiled=True)  23.4 us
    all_to_all x1, starting transfers between devices, sum_to_owners(): got = lax.all_to_all(flat, axis, 0, 0, tiled=True)  16.5 us
    all_to_all x3, waiting for transfers between devices, gather_blocks(): got = lax.all_to_all(spread, axis, 0, 0, tiled=True)  15.4 us
    all_to_all x1, starting transfers between devices, gather_stack(): return lax.all_to_all(spread, axis, 0, 0, tiled=True)  14 us
    ppermute x9, starting transfers between devices, passed_along(): lax.ppermute(shard, axis, [(i, (i + by) % length) for i in range(length)])  12.5 us
    dot_general x8, matrix products, kernel_tile_of(): lax.dot_general(left_rows, right_rows, (((1,), (1,)), ((), ())), preferre...  11.6 us
    ppermute x9, waiting for transfers between devices, passed_along(): lax.ppermute(shard, axis, [(i, (i + by) % length) for i in range(length)])  11.4 us
    dot_general x1, matrix products, prior_values(): return jnp.dot(features, prior_weight, precision=lax.Precision.HIGHEST)  10.1 us
  transfers between devices with their start and end apart: 15, of which 6 were waited for; matrix products, arithmetic and copies ran while one was open for 37% of the time, Pallas kernels for 0%

profile of v6, /device:TPU:1, one launch (start us, length us, event | category | flops | bytes accessed | tf_op | source)
XLA Modules:
  0.0 203.3 jit_solution(10371235966641557492)
XLA Ops:
  2.4 2.5 %collective-permute-start = (f32[1024,32]{0,1:T(8,128)S(1)}, f32[1024,32]{0,1:T(8,128)}, u32[]{:S(2)}, u32[]{:S(2)}) collective-permute-start(f32[1024,32]{0,1:T(8,128)S(1)} %get-tuple-element.54), channel_id=1, source_target_pairs={{0,1},{1,2},{2,3},{3,0},{4,5},{5,6},{6,7},{7,4},{8,9},{9,10},{10,1... | collective-permute-start | bytes 393224 | tf_op jit(solution)/shard_map/ppermute | solution.py:17
  5.0 3.0 %collective-permute-start.1 = (f32[1024,32]{0,1:T(8,128)S(1)}, f32[1024,32]{0,1:T(8,128)}, u32[]{:S(2)}, u32[]{:S(2)}) collective-permute-start(f32[1024,32]{0,1:T(8,128)S(1)} %get-tuple-element.54), channel_id=1, source_target_pairs={{0,2},{1,3},{2,0},{3,1},{4,6},{5,7},{6,4},{7,5},{8,10},{9,11},{10,... | collective-permute-start | bytes 393224 | tf_op jit(solution)/shard_map/ppermute | solution.py:17
  13.6 14.0 %all-to-all-start = ((bf16[64,18,512]{2,1,0:T(8,128)(2,1)}), bf16[64,18,512]{2,1,0:T(8,128)(2,1)S(1)}, u32[]{:S(2)}, u32[]{:S(2)}) async-start(bf16[64,18,512]{2,1,0:T(8,128)(2,1)} %broadcast_in_dim.59), calls=%async_computation | async-start | bytes 3145728 | tf_op jit(solution)/shard_map/all_to_all | solution.py:58
  29.6 2.1 %gather_fusion.4 = bf16[72,512]{1,0:T(8,128)(2,1)S(1)} fusion(bf16[1024,512]{1,0:T(8,128)(2,1)} %param.10, s32[1024]{0:T(1024)S(1)} %pad_clamp_fusion.2), kind=kCustom, calls=%fused_computation.4 | custom fusion | bytes 147744 | tf_op jit(solution)/shard_map/gather | solution.py:108
  35.8 10.1 %fusion.24 = f32[512,16]{0,1:T(8,128)} fusion(f32[1024,16]{0,1:T(8,128)S(1)} %copy-done.13, f32[512,1024]{1,0:T(8,128)S(1)} %fusion.117, f32[1024]{0:T(1024)S(1)} %copy-done.25), kind=kOutput, calls=%fused_computation.40 | convolution fusion | flops 102236160 | bytes 2199552 | tf_op jit(solution)/shard_map/dot_general | solution.py:44
  45.9 2.1 %fusion.118 = f32[512,1024]{1,0:T(8,128)} fusion(bf16[512,512]{1,0:T(8,128)(2,1)S(1)} %copy-done.3, bf16[1024,512]{1,0:T(8,128)(2,1)S(1)} %copy-done.1), kind=kOutput, calls=%fused_computation.203 | convolution fusion | flops 536870912 | bytes 3670016 | tf_op jit(solution)/shard_map/dot_general | solution.py:26
  53.5 4.9 %all-to-all-done = bf16[64,18,512]{2,1,0:T(8,128)(2,1)S(1)} async-done(((bf16[64,18,512]{2,1,0:T(8,128)(2,1)}), bf16[64,18,512]{2,1,0:T(8,128)(2,1)S(1)}, u32[]{:S(2)}, u32[]{:S(2)}) %all-to-all-start) | async-done | bytes 1179680 | tf_op jit(solution)/shard_map/all_to_all | solution.py:58
  60.2 3.0 %fusion = f32[1152,1024]{1,0:T(8,128)S(1)} fusion(bf16[1152,512]{1,0:T(8,128)(2,1)} %reshape.333, bf16[1024,512]{1,0:T(8,128)(2,1)} %param.10, f32[1024]{0:T(1024)S(1)} %multiply_reduce_fusion.1, f32[1152]{0:T(1024)S(1)} %add.295), kind=kOutput, calls=%fused_computation.14 | convolution fusion | flops 1211498496 | bytes 6955520 | tf_op jit(solution)/shard_map/dot_general | solution.py:26
  63.2 3.1 %fusion.1 = f32[1152,128]{1,0:T(8,128)} fusion(f32[1024,128]{0,1:T(8,128)S(1)} %bitcast.142, f32[1152,1024]{1,0:T(8,128)S(1)} %fusion), kind=kOutput, calls=%fused_computation.15 | convolution fusion | flops 909508608 | bytes 5832704 | tf_op jit(solution)/shard_map/dot_general | solution.py:35
  66.3 16.5 %all-to-all-start.1 = ((f32[64,1,2304]{2,1,0:T(1,128)}), f32[64,1,2304]{2,1,0:T(1,128)}, u32[]{:S(2)}, u32[]{:S(2)}) async-start(f32[64,1,2304]{2,1,0:T(1,128)} %bitcast.11), calls=%async_computation.1 | async-start | bytes 1179648 | tf_op jit(solution)/shard_map/all_to_all | solution.py:72
  94.3 3.7 %fusion.16 = f32[512,32]{0,1:T(8,128)} fusion(f32[1024,32]{0,1:T(8,128)S(1)} %get-tuple-element.54, f32[512,1024]{1,0:T(8,128)} %fusion.118, f32[1024]{0:T(1024)S(1)} %copy-done.27, f32[512]{0:T(512)S(1)} %multiply_reduce_fusion.3), kind=kOutput, calls=%fused_computation.31 | convolution fusion | flops 103809024 | bytes 2299904 | tf_op jit(solution)/shard_map/dot_general | solution.py:35
  102.5 2.0 reshape.339
  108.7 3.4 %all-to-all-start.2 = ((f32[4,1,576]{2,1,0:T(1,128)}), f32[4,1,576]{2,1,0:T(1,128)S(1)}, u32[]{:S(2)}, u32[]{:S(2)}) async-start(f32[4,1,576]{2,1,0:T(1,128)} %reshape.449), calls=%async_computation.2 | async-start | bytes 20480 | tf_op jit(solution)/shard_map/all_to_all | solution.py:124
  112.1 4.4 %all-to-all-done.2 = f32[4,1,576]{2,1,0:T(1,128)S(1)} async-done(((f32[4,1,576]{2,1,0:T(1,128)}), f32[4,1,576]{2,1,0:T(1,128)S(1)}, u32[]{:S(2)}, u32[]{:S(2)}) %all-to-all-start.2) | async-done | bytes 9248 | tf_op jit(solution)/shard_map/all_to_all | solution.py:124
  121.8 2.5 %collective-permute-start.5 = (f32[3,24,384]{2,1,0:T(8,128)S(1)}, f32[3,24,384]{2,1,0:T(8,128)S(1)}, u32[]{:S(2)}, u32[]{:S(2)}) collective-permute-start(f32[3,24,384]{2,1,0:T(8,128)S(1)} %pad_maximum_fusion.2), channel_id=1, source_target_pairs={{0,3},{1,0},{2,1},{3,2},{4,7},{5,4},{6,5},{7,6},{8,11},{9,8},{10,9... | collective-permute-start | bytes 331784 | tf_op jit(solution)/shard_map/ppermute | solution.py:17
  124.4 2.0 fusion.39
  126.4 2.1 %fusion.8 = f32[512,32]{0,1:T(8,128)} fusion(f32[1024,32]{0,1:T(8,128)S(1)} %get-tuple-element.54, f32[512,1024]{1,0:T(8,128)S(1)} %fusion.119, f32[512]{0:T(512)S(1)} %multiply_reduce_fusion.2, f32[1024]{0:T(1024)S(1)} %copy-done.28), kind=kOutput, calls=%fused_computation.23 | convolution fusion | flops 103809024 | bytes 2299904 | tf_op jit(solution)/shard_map/dot_general | solution.py:35
  129.5 13.8 %all-to-all-start.3 = ((f32[64,1,384]{2,1,0:T(1,128)}), f32[64,1,384]{2,1,0:T(1,128)S(1)}, u32[]{:S(2)}, u32[]{:S(2)}) async-start(f32[64,1,384]{2,1,0:T(1,128)} %broadcast_in_dim.112), calls=%async_computation.3 | async-start | bytes 196608 | tf_op jit(solution)/shard_map/all_to_all | solution.py:51
  148.8 6.7 %all-to-all-done.3 = f32[64,1,384]{2,1,0:T(1,128)S(1)} async-done(((f32[64,1,384]{2,1,0:T(1,128)}), f32[64,1,384]{2,1,0:T(1,128)S(1)}, u32[]{:S(2)}, u32[]{:S(2)}) %all-to-all-start.3) | async-done | bytes 98336 | tf_op jit(solution)/shard_map/all_to_all | solution.py:51
  157.3 6.1 %all-to-all-start.4 = ((f32[64,1,384]{2,1,0:T(1,128)}), f32[64,1,384]{2,1,0:T(1,128)S(1)}, u32[]{:S(2)}, u32[]{:S(2)}) async-start(f32[64,1,384]{2,1,0:T(1,128)} %broadcast_in_dim.115), calls=%async_computation.4 | async-start | bytes 196608 | tf_op jit(solution)/shard_map/all_to_all | solution.py:51
  163.4 2.5 %scatter_fusion.1 = f32[1024,16]{1,0:T(8,128)} fusion(f32[1024,16]{1,0:T(8,128)} %get-tuple-element.52, s32[24]{0:T(128)S(1)} %copy-done.21, f32[24,16]{1,0:T(8,128)S(1)} %copy.199), kind=kCustom, calls=%fused_computation.11 | custom fusion | flops 384 | bytes 4704 | tf_op jit(solution)/shard_map/scatter-add | solution.py:169
  168.6 7.0 %all-to-all-done.4 = f32[64,1,384]{2,1,0:T(1,128)S(1)} async-done(((f32[64,1,384]{2,1,0:T(1,128)}), f32[64,1,384]{2,1,0:T(1,128)S(1)}, u32[]{:S(2)}, u32[]{:S(2)}) %all-to-all-start.4) | async-done | bytes 98336 | tf_op jit(solution)/shard_map/all_to_all | solution.py:51
  182.1 11.3 %collective-permute-done.6 = f32[512,16]{0,1:T(8,128)S(1)} collective-permute-done((f32[512,16]{0,1:T(8,128)S(1)}, f32[512,16]{0,1:T(8,128)S(1)}, u32[]{:S(2)}, u32[]{:S(2)}) %collective-permute-start.6) | collective-permute-done | bytes 32800 | tf_op jit(solution)/shard_map/ppermute | solution.py:17
  194.7 3.5 %all-to-all-start.5 = ((f32[4,1,512]{2,1,0:T(1,128)}), f32[4,1,512]{2,1,0:T(1,128)S(1)}, u32[]{:S(2)}, u32[]{:S(2)}) async-start(f32[4,1,512]{2,1,0:T(1,128)} %broadcast_in_dim.116), calls=%async_computation.5 | async-start | bytes 16384 | tf_op jit(solution)/shard_map/all_to_all | solution.py:51
  (211 shorter events, 69.6 us)
Async XLA Ops:
  0.6 34.5 %copy-start = (bf16[512,1024]{1,0:T(8,128)(2,1)S(1)}, bf16[512,1024]{1,0:T(8,128)(2,1)}, u32[]{:S(2)}) copy-start(bf16[512,1024]{1,0:T(8,128)(2,1)} %param.17) | copy-start | bytes 3145732
  2.4 47.4 %collective-permute-start = (f32[1024,32]{0,1:T(8,128)S(1)}, f32[1024,32]{0,1:T(8,128)}, u32[]{:S(2)}, u32[]{:S(2)}) collective-permute-start(f32[1024,32]{0,1:T(8,128)S(1)} %get-tuple-element.54), channel_id=1, source_target_pairs={{0,1},{1,2},{2,3},{3,0},{4,5},{5,6},{6,7},{7,4},{8,9},{9,10},{10,1... | collective-permute-start | bytes 393224 | tf_op jit(solution)/shard_map/ppermute | solution.py:17
  5.0 44.9 %collective-permute-start.1 = (f32[1024,32]{0,1:T(8,128)S(1)}, f32[1024,32]{0,1:T(8,128)}, u32[]{:S(2)}, u32[]{:S(2)}) collective-permute-start(f32[1024,32]{0,1:T(8,128)S(1)} %get-tuple-element.54), channel_id=1, source_target_pairs={{0,2},{1,3},{2,0},{3,1},{4,6},{5,7},{6,4},{7,5},{8,10},{9,11},{10,... | collective-permute-start | bytes 393224 | tf_op jit(solution)/shard_map/ppermute | solution.py:17
  8.0 41.9 %collective-permute-start.2 = (f32[1024,32]{0,1:T(8,128)S(1)}, f32[1024,32]{0,1:T(8,128)}, u32[]{:S(2)}, u32[]{:S(2)}) collective-permute-start(f32[1024,32]{0,1:T(8,128)S(1)} %get-tuple-element.54), channel_id=1, source_target_pairs={{0,3},{1,0},{2,1},{3,2},{4,7},{5,4},{6,5},{7,6},{8,11},{9,8},{10,9... | collective-permute-start | bytes 393224 | tf_op jit(solution)/shard_map/ppermute | solution.py:17
  9.5 22.8 %copy-start.19 = (s32[24]{0:T(128)}, s32[24]{0:T(128)S(1)}, u32[]{:S(2)}) copy-start(s32[24]{0:T(128)S(1)} %get-tuple-element.67) | copy-start | bytes 292
  9.5 22.8 %copy-start.20 = (s32[24]{0:T(128)}, s32[24]{0:T(128)S(1)}, u32[]{:S(2)}) copy-start(s32[24]{0:T(128)S(1)} %get-tuple-element.68) | copy-start | bytes 292
  13.6 44.8 %all-to-all-start = ((bf16[64,18,512]{2,1,0:T(8,128)(2,1)}), bf16[64,18,512]{2,1,0:T(8,128)(2,1)S(1)}, u32[]{:S(2)}, u32[]{:S(2)}) async-start(bf16[64,18,512]{2,1,0:T(8,128)(2,1)} %broadcast_in_dim.59), calls=%async_computation | async-start | bytes 3145728 | tf_op jit(solution)/shard_map/all_to_all | solution.py:58
  27.6 24.7 %copy-start.29 = (pred[4]{0:T(512)(128)(4,1)}, pred[4]{0:T(512)(128)(4,1)S(1)}, u32[]{:S(2)}) copy-start(pred[4]{0:T(512)(128)(4,1)S(1)} %compare_and_fusion) | copy-start | bytes 16
  32.3 59.7 %copy-start.18 = (s32[1024]{0:T(1024)}, s32[1024]{0:T(1024)S(1)}, u32[]{:S(2)}) copy-start(s32[1024]{0:T(1024)S(1)} %get-tuple-element.70) | copy-start | bytes 12292
  34.1 26.1 %copy-start.26 = (f32[1024]{0:T(1024)}, f32[1024]{0:T(1024)S(1)}, u32[]{:S(2)}) copy-start(f32[1024]{0:T(1024)S(1)} %multiply_reduce_fusion.1) | copy-start | bytes 12292
  63.2 20.9 %copy-start.10 = (f32[1024,16]{0,1:T(8,128)S(1)}, f32[1024,16]{0,1:T(8,128)}, u32[]{:S(2)}) copy-start(f32[1024,16]{0,1:T(8,128)} %param.11) | copy-start | bytes 196612
  66.3 22.2 %copy-start.33 = (pred[24]{0:T(512)(128)(4,1)S(1)}, pred[24]{0:T(512)(128)(4,1)}, u32[]{:S(2)}) copy-start(pred[24]{0:T(512)(128)(4,1)} %iota_compare_fusion.2) | copy-start | bytes 76
  66.3 27.9 %copy-start.27 = (f32[1024]{0:T(1024)S(1)}, f32[1024]{0:T(1024)}, u32[]{:S(2)}) copy-start(f32[1024]{0:T(1024)} %copy-done.26) | copy-start | bytes 12292
  66.3 40.1 %all-to-all-start.1 = ((f32[64,1,2304]{2,1,0:T(1,128)}), f32[64,1,2304]{2,1,0:T(1,128)}, u32[]{:S(2)}, u32[]{:S(2)}) async-start(f32[64,1,2304]{2,1,0:T(1,128)} %bitcast.11), calls=%async_computation.1 | async-start | bytes 1179648 | tf_op jit(solution)/shard_map/all_to_all | solution.py:72
  97.9 20.0 %collective-permute-start.7 = (bf16[512,512]{1,0:T(8,128)(2,1)S(1)}, bf16[512,512]{1,0:T(8,128)(2,1)}, u32[]{:S(2)}, u32[]{:S(2)}) collective-permute-start(bf16[512,512]{1,0:T(8,128)(2,1)S(1)} %copy-done.4), channel_id=1, source_target_pairs={{0,4},{4,8},{8,12},{12,16},{16,20},{20,24},{24,28},{28,32},{32,36}... | collective-permute-start | bytes 1572872 | tf_op jit(solution)/shard_map/ppermute | solution.py:17
  108.7 7.9 %all-to-all-start.2 = ((f32[4,1,576]{2,1,0:T(1,128)}), f32[4,1,576]{2,1,0:T(1,128)S(1)}, u32[]{:S(2)}, u32[]{:S(2)}) async-start(f32[4,1,576]{2,1,0:T(1,128)} %reshape.449), calls=%async_computation.2 | async-start | bytes 20480 | tf_op jit(solution)/shard_map/all_to_all | solution.py:124
  120.9 27.0 %collective-permute-start.3 = (f32[3,24,384]{2,1,0:T(8,128)S(1)}, f32[3,24,384]{2,1,0:T(8,128)S(1)}, u32[]{:S(2)}, u32[]{:S(2)}) collective-permute-start(f32[3,24,384]{2,1,0:T(8,128)S(1)} %pad_maximum_fusion.2), channel_id=1, source_target_pairs={{0,1},{1,2},{2,3},{3,0},{4,5},{5,6},{6,7},{7,4},{8,9},{9,10},{10,1... | collective-permute-start | bytes 331784 | tf_op jit(solution)/shard_map/ppermute | solution.py:17
  121.7 26.2 %collective-permute-start.4 = (f32[3,24,384]{2,1,0:T(8,128)S(1)}, f32[3,24,384]{2,1,0:T(8,128)S(1)}, u32[]{:S(2)}, u32[]{:S(2)}) collective-permute-start(f32[3,24,384]{2,1,0:T(8,128)S(1)} %pad_maximum_fusion.2), channel_id=1, source_target_pairs={{0,2},{1,3},{2,0},{3,1},{4,6},{5,7},{6,4},{7,5},{8,10},{9,11},{10,... | collective-permute-start | bytes 331784 | tf_op jit(solution)/shard_map/ppermute | solution.py:17
  121.8 26.2 %collective-permute-start.5 = (f32[3,24,384]{2,1,0:T(8,128)S(1)}, f32[3,24,384]{2,1,0:T(8,128)S(1)}, u32[]{:S(2)}, u32[]{:S(2)}) collective-permute-start(f32[3,24,384]{2,1,0:T(8,128)S(1)} %pad_maximum_fusion.2), channel_id=1, source_target_pairs={{0,3},{1,0},{2,1},{3,2},{4,7},{5,4},{6,5},{7,6},{8,11},{9,8},{10,9... | collective-permute-start | bytes 331784 | tf_op jit(solution)/shard_map/ppermute | solution.py:17
  129.5 25.9 %all-to-all-start.3 = ((f32[64,1,384]{2,1,0:T(1,128)}), f32[64,1,384]{2,1,0:T(1,128)S(1)}, u32[]{:S(2)}, u32[]{:S(2)}) async-start(f32[64,1,384]{2,1,0:T(1,128)} %broadcast_in_dim.112), calls=%async_computation.3 | async-start | bytes 196608 | tf_op jit(solution)/shard_map/all_to_all | solution.py:51
  157.3 18.2 %all-to-all-start.4 = ((f32[64,1,384]{2,1,0:T(1,128)}), f32[64,1,384]{2,1,0:T(1,128)S(1)}, u32[]{:S(2)}, u32[]{:S(2)}) async-start(f32[64,1,384]{2,1,0:T(1,128)} %broadcast_in_dim.115), calls=%async_computation.4 | async-start | bytes 196608 | tf_op jit(solution)/shard_map/all_to_all | solution.py:51
  179.9 2.3 %collective-permute-start.8 = (f32[512,16]{0,1:T(8,128)S(1)}, f32[512,16]{0,1:T(8,128)S(1)}, u32[]{:S(2)}, u32[]{:S(2)}) collective-permute-start(f32[512,16]{0,1:T(8,128)S(1)} %fusion.58), channel_id=1, source_target_pairs={{0,4},{4,8},{8,12},{12,16},{16,20},{20,24},{24,28},{28,32},{32,36}... | collective-permute-start | bytes 98312 | tf_op jit(solution)/shard_map/ppermute | solution.py:17
  181.6 11.9 %collective-permute-start.6 = (f32[512,16]{0,1:T(8,128)S(1)}, f32[512,16]{0,1:T(8,128)S(1)}, u32[]{:S(2)}, u32[]{:S(2)}) collective-permute-start(f32[512,16]{0,1:T(8,128)S(1)} %fusion.60), channel_id=1, source_target_pairs={{0,8},{4,12},{8,16},{12,20},{16,24},{20,28},{24,32},{28,36},{32,40... | collective-permute-start | bytes 98312 | tf_op jit(solution)/shard_map/ppermute | solution.py:17
  194.7 7.9 %all-to-all-start.5 = ((f32[4,1,512]{2,1,0:T(1,128)}), f32[4,1,512]{2,1,0:T(1,128)S(1)}, u32[]{:S(2)}, u32[]{:S(2)}) async-start(f32[4,1,512]{2,1,0:T(1,128)} %broadcast_in_dim.116), calls=%async_computation.5 | async-start | bytes 16384 | tf_op jit(solution)/shard_map/all_to_all | solution.py:51
  (30 other events, 299.1 us)
